TPU v7x, 256 devices: a whole 4x4x8 slice. The times are simulated.
256 devices in a mesh: seq: 32 (over y, x, core), tp: 8 (over z).
Axes of the slice: x: 4, y: 4, z: 8, core: 2. Of those that a mesh axis runs over, the one named last changes fastest.
Arguments:
- x_resid: bfloat16 [4096, 2880], P('seq', 'tp'), may hold values from -6 to 6
- q_new: bfloat16 [4096, 4096], P('seq', 'tp'), may hold values from -10 to 12
- kv_new: bfloat16 [4096, 8, 128], P('seq', 'tp'), may hold values from -4 to 4
- kv_cache: bfloat16 [1024, 32, 8, 128], P('seq', None, 'tp'), may hold values from -4 to 11.5
- cache_len: int32 [32], replicated, may hold values from 0 to 1024, as said below
- page_table: int32 [32, 32], replicated, may hold values from 0 to 1023, as said below
- sinks: float32 [64], P('tp'), may hold values from 0 to 8
- out_weight: bfloat16 [4096, 2880], P('tp'), may hold values from -0.09375 to 0.09375
- norm_gain: float32 [2880], replicated, may hold values from 0.1 to 1.9
- routes: int32 [4096, 4], P('seq'), may hold values from 0 to 31, all different within a row; in each aligned block of 128 rows (0 to 127, 128 to 255, ...) at most 32 rows name the same one
- route_wt: float32 [4096, 4], P('seq'), may hold values from 0.05 to 0.5
- w_gate: bfloat16 [32, 2880, 2880], P('seq', None, 'tp'), may hold values from -0.109375 to 0.109375
- w_up: bfloat16 [32, 2880, 2880], P('seq', None, 'tp'), may hold values from -0.109375 to 0.109375
- w_down: bfloat16 [32, 2880, 2880], P('seq', 'tp'), may hold values from -0.109375 to 0.109375
Outputs:
- attended: bfloat16 [4096, 4096], P('seq', 'tp')
- output: bfloat16 [4096, 2880], P('seq', 'tp')
Inputs may be any that keep to these rules, and one draw needn't show every extreme that they name: `routes`: each row names 4 different experts; in each aligned block of 128 rows no expert is named by more than 32 rows. `cache_len`: the largest is exactly 1024. `page_table`: every pool page appears exactly once; pool pages d * 32 to (d + 1) * 32 - 1 hold exactly 1 pages of each request.
All inputs are finite; a program needn't handle non-finite values.
Results may differ from a plain program's by a relative error of at most 0.02.
Values may be sent and summed in bfloat16 or wider, within the bound.
No kernel may reach another device: no remote copies, remote signals or barrier semaphores. Data moves between devices by JAX's collectives and lax.ppermute only.
A program may use at most 128 MiB of HBM per device.

v0:
```python
import math

import jax
import jax.numpy as jnp
from jax import lax
from jax.sharding import PartitionSpec as P

D = 2880
NEW = 128


rope_base = 150000.0
neg_big = -1e30
norm_eps = 1e-05


def rotate(values, where):
    half = values.shape[-1] // 2
    freq = rope_base ** (-jnp.arange(half, dtype=jnp.float32) * 2.0 / values.shape[-1])
    angle = where.astype(jnp.float32)[:, None] * freq[None, :]
    cosine = jnp.cos(angle)[:, None, :]
    sine = jnp.sin(angle)[:, None, :]
    first = values[..., :half]
    second = values[..., half:]
    return jnp.concatenate([first * cosine - second * sine, first * sine + second * cosine], -1)


def absorb(state, queries, keys, values, allowed, group):
    best, total, summed = state
    scores = jnp.einsum(
        "hqd,khd->hqk", queries, keys, preferred_element_type=jnp.float32
    ) * queries.shape[-1] ** (-0.5)
    wide = jnp.repeat(allowed, group, axis=0)
    scores = jnp.where(wide[None], scores, neg_big)
    peak = jnp.maximum(best, jnp.max(scores, -1))
    factor = jnp.exp(best - peak)
    expo = jnp.exp(scores - peak[..., None])
    total = total * factor + jnp.sum(expo, -1)
    summed = summed * factor[..., None] + jnp.einsum(
        "hqk,khd->hqd", expo.astype(jnp.bfloat16), values, preferred_element_type=jnp.float32
    )
    return (peak, total, summed)


def absorb_pages(state, queries, pages, page_req, page_pos, row_req, row_len, group, block_pages):
    count, page, local_kv, width = pages.shape
    head = width // 2
    step = math.gcd(count, block_pages)
    blocks = count // step
    pages_b = pages.reshape(blocks, step, page, local_kv, width)
    req_b = page_req.reshape(blocks, step)
    pos_b = page_pos.reshape(blocks, step, page)

    def one_block(carry, item):
        block, owners, spots = item
        flat_keys = block.reshape(step * page, local_kv, width)
        allowed = (owners[None, :, None] == row_req[:, None, None]) & (
            spots[None] < row_len[:, None, None]
        )
        allowed = allowed.reshape(row_req.shape[0], step * page)
        return (
            absorb(carry, queries, flat_keys[..., :head], flat_keys[..., head:], allowed, group),
            None,
        )

    state, _ = lax.scan(one_block, state, (pages_b, req_b, pos_b))
    return state


def per_device(
    x_resid,
    q_new,
    kv_new,
    kv_cache,
    cache_len,
    page_table,
    sinks,
    out_weight,
    norm_gain,
    routes,
    route_wt,
    w_gate,
    w_up,
    w_down,
):
    seq_count = lax.axis_size("seq")
    seq_here = lax.axis_index("seq")
    tp_here = lax.axis_index("tp")
    rows, cols = x_resid.shape
    local_kv = kv_new.shape[1]
    head = kv_new.shape[2] // 2
    local_q = q_new.shape[1] // head
    group = local_q // local_kv
    slots = kv_cache.shape[0]
    page = kv_cache.shape[1]
    requests, max_pages = page_table.shape
    topk = routes.shape[1]
    row_ids = seq_here * rows + jnp.arange(rows, dtype=jnp.int32)
    row_req = row_ids // NEW
    row_off = row_ids % NEW
    request_ids = jnp.arange(requests, dtype=jnp.int32)
    pick = (row_req[:, None] == request_ids[None, :]).astype(jnp.int32)
    row_len = jnp.sum(pick * cache_len[None, :], 1)
    where = row_len + row_off
    rotated = rotate(q_new.reshape(rows, local_q, head).astype(jnp.float32), where).astype(
        jnp.bfloat16
    )
    queries = (
        rotated.reshape(rows, local_kv, group, head)
        .transpose(1, 0, 2, 3)
        .reshape(local_kv, rows * group, head)
    )
    fresh_keys = rotate(kv_new[..., :head].astype(jnp.float32), where).astype(jnp.bfloat16)
    fresh = jnp.concatenate([fresh_keys, kv_new[..., head:]], -1)
    sink_rows = jnp.broadcast_to(
        sinks.reshape(local_kv, 1, group), (local_kv, rows, group)
    ).reshape(local_kv, rows * group)
    state = (
        sink_rows,
        jnp.ones_like(sink_rows),
        jnp.zeros((local_kv, rows * group, head), jnp.float32),
    )
    own_allowed = (row_req[None, :] == row_req[:, None]) & (row_ids[None, :] <= row_ids[:, None])
    state = absorb(state, queries, fresh[..., :head], fresh[..., head:], own_allowed, group)
    piece = lax.all_gather(kv_cache, "seq", axis=0, tiled=True)
    count = piece.shape[0]
    ids = jnp.arange(count, dtype=jnp.int32)
    match = (page_table[None, :, :] == ids[:, None, None]).astype(jnp.int32)
    page_req = jnp.sum(match * request_ids[None, :, None], (1, 2))
    page_num = jnp.sum(match * jnp.arange(max_pages, dtype=jnp.int32)[None, None, :], (1, 2))
    page_pos = page_num[:, None] * page + jnp.arange(page, dtype=jnp.int32)[None, :]
    state = absorb_pages(state, queries, piece, page_req, page_pos, row_req, row_len, group, slots)
    best, total, summed = state
    attended = (summed / total[..., None]).astype(jnp.bfloat16)
    attended = (
        attended.reshape(local_kv, rows, group, head)
        .transpose(1, 0, 2, 3)
        .reshape(rows, local_q * head)
    )
    partial_value = jnp.dot(attended, out_weight, preferred_element_type=jnp.float32)
    gain_here = lax.dynamic_slice_in_dim(norm_gain, tp_here * cols, cols)
    column_sums = lax.psum_scatter(
        partial_value.astype(jnp.bfloat16), "tp", scatter_dimension=1, tiled=True
    ).astype(jnp.float32)
    resid = (x_resid.astype(jnp.float32) + column_sums).astype(jnp.bfloat16)
    resid_wide = resid.astype(jnp.float32)
    squares = lax.psum(jnp.sum(resid_wide * resid_wide, 1), "tp")
    scale_rows = lax.rsqrt(squares / D + norm_eps)
    normed_cols = (resid_wide * scale_rows[:, None] * gain_here[None, :]).astype(jnp.bfloat16)
    normed_full = None
    local_e = w_gate.shape[0]
    experts_all = local_e * seq_count
    cap = 2 * rows * topk // experts_all
    flat_routes = routes.reshape(-1)
    onehot = (flat_routes[:, None] == jnp.arange(experts_all, dtype=jnp.int32)[None, :]).astype(
        jnp.int32
    )
    rank = jnp.sum(onehot * (jnp.cumsum(onehot, 0) - 1), 1)
    slot = flat_routes * cap + rank
    source = (
        jnp.full((experts_all * cap,), rows, jnp.int32)
        .at[slot]
        .set(jnp.arange(rows * topk, dtype=jnp.int32) // topk)
    )
    normed_full = lax.all_gather(normed_cols, "tp", axis=1, tiled=True)
    padded = jnp.concatenate([normed_full, jnp.zeros((1, D), jnp.bfloat16)], 0)
    outgoing_rows = padded[source].reshape(seq_count, local_e * cap, D)
    incoming_rows = lax.all_to_all(outgoing_rows, "seq", split_axis=0, concat_axis=0, tiled=True)
    arrived = incoming_rows.reshape(seq_count, local_e, cap, D)
    hidden = jnp.einsum("sexd,edf->sexf", arrived, w_gate, preferred_element_type=jnp.float32)
    lin = jnp.einsum("sexd,edf->sexf", arrived, w_up, preferred_element_type=jnp.float32)
    act = (hidden * jax.nn.sigmoid(1.702 * hidden) * (lin + 1.0)).astype(jnp.bfloat16)
    down = jnp.einsum("sexf,efd->sexd", act, w_down, preferred_element_type=jnp.float32)
    expert_out = lax.psum_scatter(down.astype(jnp.bfloat16), "tp", scatter_dimension=3, tiled=True)
    returned = lax.all_to_all(
        expert_out.reshape(seq_count, local_e * cap, cols),
        "seq",
        split_axis=0,
        concat_axis=0,
        tiled=True,
    )
    taken = (
        returned.reshape(experts_all * cap, cols)[slot]
        .reshape(rows, topk, cols)
        .astype(jnp.float32)
    )
    mixture = jnp.sum(route_wt[..., None] * taken, 1)
    output = (resid_wide + mixture).astype(jnp.bfloat16)
    return (attended, output)


def solution(mesh):
    in_specs = (
        P("seq", "tp"),
        P("seq", "tp"),
        P("seq", "tp", None),
        P("seq", None, "tp", None),
        P(),
        P(),
        P("tp"),
        P("tp", None),
        P(),
        P("seq", None),
        P("seq", None),
        P("seq", None, "tp"),
        P("seq", None, "tp"),
        P("seq", "tp", None),
    )
    out_specs = (P("seq", "tp"), P("seq", "tp"))
    return jax.shard_map(
        per_device, mesh=mesh, in_specs=in_specs, out_specs=out_specs, check_vma=False
    )
```

profile of v0, /device:TPU:1, one launch (start us, length us, event | category | flops | bytes accessed | tf_op | source)
XLA Modules:
  0.0 694.3 jit_solution(1581634424990804674)
XLA Ops:
  22.0 50.6 %all-gather.2.cloned.1.call-done = bf16[1024,32,1,128]{3,1,2,0:T(8,128)(2,1)} async-done(((bf16[32,32,1,128]{3,1,2,0:T(8,128)(2,1)}), bf16[1024,32,1,128]{3,1,2,0:T(8,128)(2,1)}) %all-gather.2.cloned.1.call-update) | async-done | bytes 8388624 | tf_op jit(solution)/shard_map/all_gather | solution.py:125
  72.6 257.6 %while.15 = (s32[]{:T(128)}, f32[1,1024]{1,0:T(1,128)S(1)}, f32[1,1024]{1,0:T(1,128)S(1)}, f32[1,1024,64]{1,2,0:T(8,128)S(1)}, s32[32,32]{1,0:T(8,128)}, /*index...) while((s32[]{:T(128)}, f32[1,1024]{1,0:T(1,128)S(1)}, ...), condition=%wide.region_8.9_spmd.clone, body=%wide.region_5.8_spmd.clone.sunk | while | flops 276176896 | bytes 19101692 | solution.py:66
  77.2 1.8 fusion.87
  85.3 1.8 fusion.87
  93.3 1.8 fusion.87
  101.4 1.8 fusion.87
  109.4 1.8 fusion.87
  117.5 1.8 fusion.87
  125.5 1.8 fusion.87
  149.7 1.8 fusion.87
  173.8 1.8 fusion.87
  181.9 1.8 fusion.87
  198.0 1.8 fusion.87
  206.0 1.8 fusion.87
  230.2 1.8 fusion.87
  335.6 2.4 scatter_custom_fusion
  338.1 27.3 %reduce-scatter.9.cloned.1.call-done = bf16[128,360]{0,1:T(8,128)(2,1)} async-done(((bf16[128,2880]{0,1:T(8,128)(2,1)}), bf16[128,360]{0,1:T(8,128)(2,1)}) %reduce-scatter.9.cloned.1.call-update) | async-done | bytes 92176
  366.5 11.4 %psum.7 = f32[128]{0:T(128)S(1)} all-reduce(f32[128]{0:T(128)S(1)} %fusion.41), channel_id=1, replica_groups=mesh['seq'=32,'tp'=8] {'tp'}, use_global_device_ids=true, to_apply=%region_11.12 | all-reduce | flops 128 | bytes 1024 | tf_op jit(solution)/shard_map/psum | solution.py:147
  378.1 20.4 %all_gather.7 = bf16[128,2880]{0,1:T(8,128)(2,1)S(1)} all-gather(bf16[128,360]{0,1:T(8,128)(2,1)S(1)} %copy.120), channel_id=1, replica_groups=mesh['seq'=32,'tp'=8] {'tp'}, dimensions={1}, use_global_device_ids=true | all-gather | bytes 829440 | tf_op jit(solution)/shard_map/all_gather | solution.py:165
  399.0 6.5 gather_fusion
  405.6 92.4 %all_to_all.10 = bf16[32,32,2880]{2,1,0:T(8,128)(2,1)S(1)} all-to-all(bf16[32,32,2880]{2,1,0:T(8,128)(2,1)} %bitcast.174), channel_id=1, replica_groups=mesh['seq'=32,'tp'=8] {'seq'}, dimensions={0} | all-to-all | bytes 11796480 | tf_op jit(solution)/shard_map/all_to_all | solution.py:168
  498.0 2.6 copy-done.2
  500.6 4.5 fusion.18
  505.1 12.0 %convert_bitcast_fusion = bf16[32,1,32,2880]{3,2,0,1:T(8,128)(2,1)} fusion(bf16[1,360,2880]{2,1,0:T(8,128)(2,1)} %param.29, bf16[32,32,2880]{2,1,0:T(8,128)(2,1)} %copy-done.2, bf16[1,2880,360]{1,2,0:T(8,128)(2,1)} %param.28, f32[32,32,360]{2,1,0:T(8,128)} %fusion.18), kind=kOutput, calls=%fused_computation.28 | convolution fusion | flops 4252631040 | bytes 17418240 | tf_op jit(solution)/shard_map/sexf,efd->sexd/dot_general | solution.py:173
  517.1 32.1 %copy.127 = bf16[32,1,32,2880]{2,0,1,3:T(8,128)(2,1)} copy(bf16[32,1,32,2880]{3,2,0,1:T(8,128)(2,1)} %convert_bitcast_fusion) | data formatting | bytes 11796480
  549.2 32.1 %reshape.566 = bf16[2880,1024]{1,0:T(8,128)(2,1)} reshape(bf16[2880,1,32,32]{3,2,1,0:T(8,128)(2,1)} %bitcast.171) | data formatting | bytes 11796480
  581.3 68.0 %reduce-scatter.7.cloned.1.call-done = bf16[360,1024]{1,0:T(8,128)(2,1)} async-done(((bf16[2880,1024]{1,0:T(8,128)(2,1)}), bf16[360,1024]{1,0:T(8,128)(2,1)}) %reduce-scatter.7.cloned.1.call-update) | async-done | bytes 737296
  649.3 4.6 reshape.567
  653.9 5.3 copy.128
  659.2 7.6 %all-to-all-start.1 = ((bf16[32,32,360]{2,1,0:T(8,128)(2,1)}), bf16[32,32,360]{2,1,0:T(8,128)(2,1)}, u32[]{:S(2)}, u32[]{:S(2)}) async-start(bf16[32,32,360]{2,1,0:T(8,128)(2,1)} %bitcast.176), calls=%async_computation.1 | async-start | bytes 1572864 | tf_op jit(solution)/shard_map/all_to_all | solution.py:175
  667.6 13.5 %all-to-all-done.1 = bf16[32,32,360]{2,1,0:T(8,128)(2,1)} async-done(((bf16[32,32,360]{2,1,0:T(8,128)(2,1)}), bf16[32,32,360]{2,1,0:T(8,128)(2,1)}, u32[]{:S(2)}, u32[]{:S(2)}) %all-to-all-start.1) | async-done | bytes 737312 | tf_op jit(solution)/shard_map/all_to_all | solution.py:175
  681.2 3.0 gather_fusion.1
  (588 shorter events, 257.4 us)
Async XLA Ops:
  7.2 323.5 %copy-start = (bf16[512,2880]{0,1:T(8,128)(2,1)S(1)}, bf16[512,2880]{0,1:T(8,128)(2,1)}, u32[]{:S(2)}) copy-start(bf16[512,2880]{0,1:T(8,128)(2,1)} %param.23) | copy-start | bytes 8847364
  7.2 65.4 %all-gather.2.cloned.1.call-start = ((), (), s32[]{:S(2)}) async-start(), calls=%async_computation.4 | async-start | bytes 8650752 | tf_op jit(solution)/shard_map/all_gather | solution.py:125
  7.9 357.4 %reduce-scatter.9.cloned.1.call-start = ((), (), s32[]{:S(2)}) async-start(), calls=%async_computation.6 | async-start | bytes 829440
  10.0 1.4 copy-start.6
  10.0 1.4 copy-start.8
  330.2 2.4 copy-start.5
  330.2 2.6 copy-start.4
  330.6 68.3 %copy-start.3 = (bf16[128,512]{1,0:T(8,128)(2,1)}, bf16[128,512]{1,0:T(8,128)(2,1)S(1)}, u32[]{:S(2)}) copy-start(bf16[128,512]{1,0:T(8,128)(2,1)S(1)} %reshape_transpose_reshape.4) | copy-start | bytes 393220
  332.5 316.8 %reduce-scatter.7.cloned.1.call-start = ((), (), s32[]{:S(2)}) async-start(), calls=%async_computation.5 | async-start | bytes 6635520
  405.6 95.0 %copy-start.9 = (bf16[1,2880,360]{1,2,0:T(8,128)(2,1)S(1)}, bf16[1,2880,360]{1,2,0:T(8,128)(2,1)}, u32[]{:S(2)}) copy-start(bf16[1,2880,360]{1,2,0:T(8,128)(2,1)} %param.27) | copy-start | bytes 6220804
  498.0 2.6 copy-start.2
  581.3 85.5 %copy-start.7 = (f32[128,4]{0,1:T(4,128)S(1)}, f32[128,4]{0,1:T(4,128)}, u32[]{:S(2)}) copy-start(f32[128,4]{0,1:T(4,128)} %param.26) | copy-start | bytes 6148
  653.9 33.9 %copy-start.1 = (bf16[512,2880]{0,1:T(8,128)(2,1)S(1)}, bf16[512,2880]{0,1:T(8,128)(2,1)}, u32[]{:S(2)}) copy-start(bf16[512,2880]{0,1:T(8,128)(2,1)} %param.23) | copy-start | bytes 8847364
  659.2 21.9 %all-to-all-start.1 = ((bf16[32,32,360]{2,1,0:T(8,128)(2,1)}), bf16[32,32,360]{2,1,0:T(8,128)(2,1)}, u32[]{:S(2)}, u32[]{:S(2)}) async-start(bf16[32,32,360]{2,1,0:T(8,128)(2,1)} %bitcast.176), calls=%async_computation.1 | async-start | bytes 1572864 | tf_op jit(solution)/shard_map/all_to_all | solution.py:175
Sparse Core Ops, SparseCore 0:
  10.5 61.9 all-gather.1
  332.6 32.6 reduce-scatter.8
  581.4 67.8 reduce-scatter.6
where the time goes:
time: 701 us; the launch traced here: 694 us
  local copies, waits for them, and re-layouts  239 us (34%)
  waiting for transfers between devices  160 us (23%)
  blocking collectives  124 us (18%)
  matrix products  106 us (15%)
  other arithmetic  40.1 us (6%)
  between operations  14.1 us (2%)
  starting transfers between devices  7.76 us (1%)
    unnamed x5, waiting for transfers between devices  96 us
    all_to_all x1, blocking collectives, per_device(): lax.all_to_all(outgoing_rows, 'seq', split_axis=0, concat_axis=0, tiled=T...  92.4 us
    unnamed x30, local copies, waits for them, and re-layouts  80.4 us
    dot_general x33, matrix products, absorb(): jnp.einsum('hqd,khd->hqk', queries, keys, preferred_element_type=jnp.floa...  59.8 us
    dynamic_slice x64, local copies, waits for them, and re-layouts, absorb_pages(): state, _ = lax.scan(one_block, state, (pages_b, req_b, pos_b))  54.2 us
    reshape x64, local copies, waits for them, and re-layouts, absorb(): scores = jnp.where(wide[None], scores, neg_big)  52.6 us
    all_gather x1, waiting for transfers between devices, per_device(): piece = lax.all_gather(kv_cache, 'seq', axis=0, tiled=True)  50.6 us
    dot_general x33, matrix products, absorb(): jnp.einsum('hqk,khd->hqd', expo.astype(jnp.bfloat16), values, preferred_e...  28.3 us
  transfers between devices with their start and end apart: 4, of which 4 were waited for; matrix products, arithmetic and copies ran while one was open for 3% of the time, Pallas kernels for 0%

commit v1 on v0

v1 whole, which is shorter than its diff:
```python
import jax
import jax.numpy as jnp
from jax import lax
from jax.sharding import PartitionSpec as P

D = 2880
NEW = 128


rope_base = 150000.0
neg_big = -1e30
norm_eps = 1e-05


def rotate(values, where):
    half = values.shape[-1] // 2
    freq = rope_base ** (-jnp.arange(half, dtype=jnp.float32) * 2.0 / values.shape[-1])
    angle = where.astype(jnp.float32)[:, None] * freq[None, :]
    cosine = jnp.cos(angle)[:, None, :]
    sine = jnp.sin(angle)[:, None, :]
    first = values[..., :half]
    second = values[..., half:]
    return jnp.concatenate([first * cosine - second * sine, first * sine + second * cosine], -1)


def per_device(
    x_resid,
    q_new,
    kv_new,
    kv_cache,
    cache_len,
    page_table,
    sinks,
    out_weight,
    norm_gain,
    routes,
    route_wt,
    w_gate,
    w_up,
    w_down,
):
    seq_count = lax.axis_size("seq")
    seq_here = lax.axis_index("seq")
    rows, cols = x_resid.shape
    local_kv = kv_new.shape[1]
    head = kv_new.shape[2] // 2
    local_q = q_new.shape[1] // head
    group = local_q // local_kv
    slots = kv_cache.shape[0]
    page = kv_cache.shape[1]
    requests, max_pages = page_table.shape
    topk = routes.shape[1]
    assert rows == NEW and requests == seq_count and max_pages == seq_count

    length = cache_len[seq_here]
    where = length + jnp.arange(rows, dtype=jnp.int32)
    queries = rotate(q_new.reshape(rows, local_q, head).astype(jnp.float32), where).astype(
        jnp.bfloat16
    )
    fresh_keys = rotate(kv_new[..., :head].astype(jnp.float32), where).astype(jnp.bfloat16)
    fresh_vals = kv_new[..., head:]

    home = page_table // slots
    mine = home == seq_here
    slot_of = jnp.sum(jnp.where(mine, page_table % slots, 0), 1)
    outgoing = kv_cache[slot_of]
    incoming = lax.all_to_all(outgoing, "seq", split_axis=0, concat_axis=0, tiled=True)
    own_home = home[seq_here]
    page_ids = jnp.arange(max_pages, dtype=jnp.int32)
    src_ids = jnp.arange(seq_count, dtype=jnp.int32)
    page_of_src = jnp.sum(
        jnp.where(own_home[None, :] == src_ids[:, None], page_ids[None, :], 0), 1
    )
    spots = page_of_src[:, None] * page + jnp.arange(page, dtype=jnp.int32)[None, :]
    cache_ok = (spots < length).reshape(seq_count * page)
    cache_keys = incoming[..., :head].reshape(seq_count * page, local_kv, head)
    cache_vals = incoming[..., head:].reshape(seq_count * page, local_kv, head)

    q_g = queries.reshape(rows, local_kv, group, head)
    scale = head ** (-0.5)
    s_cache = jnp.einsum(
        "ngqd,kgd->gqnk", q_g, cache_keys, preferred_element_type=jnp.float32
    ) * scale
    s_cache = jnp.where(cache_ok[None, None, None, :], s_cache, neg_big)
    s_new = jnp.einsum(
        "ngqd,kgd->gqnk", q_g, fresh_keys, preferred_element_type=jnp.float32
    ) * scale
    tok = jnp.arange(rows, dtype=jnp.int32)
    causal = tok[None, :] <= tok[:, None]
    s_new = jnp.where(causal[None, None], s_new, neg_big)
    sink = sinks.reshape(local_kv, group)[:, :, None]
    top = jnp.maximum(jnp.maximum(jnp.max(s_cache, -1), jnp.max(s_new, -1)), sink)
    e_cache = jnp.exp(s_cache - top[..., None])
    e_new = jnp.exp(s_new - top[..., None])
    total = jnp.sum(e_cache, -1) + jnp.sum(e_new, -1) + jnp.exp(sink - top)
    summed = jnp.einsum(
        "gqnk,kgd->gqnd", e_cache.astype(jnp.bfloat16), cache_vals,
        preferred_element_type=jnp.float32,
    ) + jnp.einsum(
        "gqnk,kgd->gqnd", e_new.astype(jnp.bfloat16), fresh_vals,
        preferred_element_type=jnp.float32,
    )
    attended = (summed / total[..., None]).astype(jnp.bfloat16)
    attended = attended.transpose(2, 0, 1, 3).reshape(rows, local_q * head)

    partial_value = jnp.dot(attended, out_weight, preferred_element_type=jnp.float32)
    column_sums = lax.psum_scatter(
        partial_value.astype(jnp.bfloat16), "tp", scatter_dimension=1, tiled=True
    ).astype(jnp.float32)
    resid = (x_resid.astype(jnp.float32) + column_sums).astype(jnp.bfloat16)
    resid_wide = resid.astype(jnp.float32)
    resid_full = lax.all_gather(resid, "tp", axis=1, tiled=True).astype(jnp.float32)
    squares = jnp.sum(resid_full * resid_full, 1)
    scale_rows = lax.rsqrt(squares / D + norm_eps)
    normed_full = (resid_full * scale_rows[:, None] * norm_gain[None, :]).astype(jnp.bfloat16)

    local_e = w_gate.shape[0]
    experts_all = local_e * seq_count
    cap = 2 * rows * topk // experts_all
    flat_routes = routes.reshape(-1)
    onehot = (flat_routes[:, None] == jnp.arange(experts_all, dtype=jnp.int32)[None, :]).astype(
        jnp.int32
    )
    rank = jnp.sum(onehot * (jnp.cumsum(onehot, 0) - 1), 1)
    slot = flat_routes * cap + rank
    source = (
        jnp.full((experts_all * cap,), rows, jnp.int32)
        .at[slot]
        .set(jnp.arange(rows * topk, dtype=jnp.int32) // topk)
    )
    padded = jnp.concatenate([normed_full, jnp.zeros((1, D), jnp.bfloat16)], 0)
    outgoing_rows = padded[source].reshape(seq_count, local_e * cap, D)
    incoming_rows = lax.all_to_all(outgoing_rows, "seq", split_axis=0, concat_axis=0, tiled=True)
    arrived = incoming_rows.reshape(seq_count, local_e, cap, D)
    hidden = jnp.einsum("sexd,edf->sexf", arrived, w_gate, preferred_element_type=jnp.float32)
    lin = jnp.einsum("sexd,edf->sexf", arrived, w_up, preferred_element_type=jnp.float32)
    act = (hidden * jax.nn.sigmoid(1.702 * hidden) * (lin + 1.0)).astype(jnp.bfloat16)
    down = jnp.einsum("sexf,efd->sexd", act, w_down, preferred_element_type=jnp.float32)
    expert_out = lax.psum_scatter(down.astype(jnp.bfloat16), "tp", scatter_dimension=3, tiled=True)
    returned = lax.all_to_all(
        expert_out.reshape(seq_count, local_e * cap, cols),
        "seq",
        split_axis=0,
        concat_axis=0,
        tiled=True,
    )
    taken = (
        returned.reshape(experts_all * cap, cols)[slot]
        .reshape(rows, topk, cols)
        .astype(jnp.float32)
    )
    mixture = jnp.sum(route_wt[..., None] * taken, 1)
    output = (resid_wide + mixture).astype(jnp.bfloat16)
    return (attended, output)


def solution(mesh):
    in_specs = (
        P("seq", "tp"),
        P("seq", "tp"),
        P("seq", "tp", None),
        P("seq", None, "tp", None),
        P(),
        P(),
        P("tp"),
        P("tp", None),
        P(),
        P("seq", None),
        P("seq", None),
        P("seq", None, "tp"),
        P("seq", None, "tp"),
        P("seq", "tp", None),
    )
    out_specs = (P("seq", "tp"), P("seq", "tp"))
    return jax.shard_map(
        per_device, mesh=mesh, in_specs=in_specs, out_specs=out_specs, check_vma=False
    )
```

time: 701 us -> 384 us (0.55)
  local copies, waits for them, and re-layouts: 239 us -> 99.1 us
  matrix products: 106 us -> 23.8 us
  waiting for transfers between devices: 160 us -> 111 us
  other arithmetic: 40.1 us -> 8.8 us
  blocking collectives: 124 us -> 109 us
  starting transfers between devices: 7.76 us -> 16.3 us
    dot_general x66 -> x4, matrix products: 88.1 us -> 5.49 us  [the longest x1 2.48 us: per_device(): jnp.einsum('ngqd,kgd->gqnk', q_g, fresh_keys, preferred_element_type=jnp....]
    dynamic_slice x65 -> x1, local copies, waits for them, and re-layouts: 55 us -> 1.24 us  [per_device(): length = cache_len[seq_here]]
    reshape x65 -> x0, local copies, waits for them, and re-layouts: 53.2 us -> none  [the longest x64 52.6 us: absorb(): scores = jnp.where(wide[None], scores, neg_big)]
    all_gather x1 -> x0, waiting for transfers between devices: 50.6 us -> none  [per_device(): piece = lax.all_gather(kv_cache, 'seq', axis=0, tiled=True)]
    eq x32 -> x1, local copies, waits for them, and re-layouts: 22.3 us -> 0.01 us  [per_device(): own_home[None, :] == src_ids[:, None]]
    reduce_sum x36 -> x4, other arithmetic: 22.5 us -> 1.35 us  [the longest x2 1.01 us: per_device(): total = jnp.sum(e_cache, -1) + jnp.sum(e_new, -1) + jnp.exp(sink - top)]
    psum x1 -> x0, blocking collectives: 11.4 us -> none  [per_device(): squares = lax.psum(jnp.sum(resid_wide * resid_wide, 1), 'tp')]
    all_to_all x0 -> x1, starting transfers between devices: none -> 8.58 us  [per_device(): lax.all_to_all(outgoing, 'seq', split_axis=0, concat_axis=0, tiled=True)]
  transfers between devices with their start and end apart: 4 -> 4, of which waited for: 4 -> 3; matrix products, arithmetic and copies ran while one was open for 3% -> 4% of each run, Pallas kernels for 0% -> 0%
where the time goes in v1:
time: 384 us; the launch traced here: 383 us
  waiting for transfers between devices  111 us (29%)
  blocking collectives  109 us (28%)
  local copies, waits for them, and re-layouts  99.1 us (26%)
  matrix products  23.8 us (6%)
  starting transfers between devices  16.3 us (4%)
  between operations  14.4 us (4%)
  other arithmetic  8.8 us (2%)
    unnamed x4, waiting for transfers between devices  98 us
    all_to_all x1, blocking collectives, per_device(): lax.all_to_all(outgoing_rows, 'seq', split_axis=0, concat_axis=0, tiled=T...  89 us
    unnamed x36, local copies, waits for them, and re-layouts  77.7 us
    all_gather x1, blocking collectives, per_device(): lax.all_gather(resid, 'tp', axis=1, tiled=True).astype(jnp.float32)  19.9 us
    all_to_all x1, waiting for transfers between devices, per_device(): lax.all_to_all(expert_out.reshape(seq_count, local_e * cap, cols), 'seq',...  13.4 us
    dot_general x1, matrix products, per_device(): jnp.einsum('sexf,efd->sexd', act, w_down, preferred_element_type=jnp.floa...  12 us
    all_to_all x1, starting transfers between devices, per_device(): lax.all_to_all(outgoing, 'seq', split_axis=0, concat_axis=0, tiled=True)  8.58 us
  transfers between devices with their start and end apart: 4, of which 3 were waited for; matrix products, arithmetic and copies ran while one was open for 4% of the time, Pallas kernels for 0%

profile of v1, /device:TPU:1, one launch (start us, length us, event | category | flops | bytes accessed | tf_op | source)
XLA Modules:
  0.0 382.7 jit_solution(14610481318534463630)
XLA Ops:
  7.2 1.0 add_select_fusion.1
  8.2 2.2 gather_fusion
  10.4 8.6 %all-to-all-start = ((bf16[32,32,1,128]{3,1,2,0:T(8,128)(2,1)}), bf16[32,32,1,128]{3,1,2,0:T(8,128)(2,1)S(1)}, u32[]{:S(2)}, u32[]{:S(2)}) async-start(bf16[32,32,1,128]{3,1,2,0:T(8,128)(2,1)} %bitcast.5), calls=%async_computation | async-start | bytes 524288 | tf_op jit(solution)/shard_map/all_to_all | solution.py:67
  19.1 1.2 dynamic_slice.7
  21.0 1.0 copy.56
  22.1 1.3 add_compare_fusion
  25.3 1.3 lt.56
  26.7 2.5 fusion.72
  29.3 1.6 bitcast_reduce_fusion
  31.1 0.9 fusion.1
  32.0 1.1 fusion.9
  33.6 1.8 convolution_convert_fusion
  35.9 1.2 reduce-window.6
  37.7 2.4 scatter_custom_fusion
  40.2 31.4 %reduce-scatter.9.cloned.1.call-done = bf16[128,360]{0,1:T(8,128)(2,1)} async-done(((bf16[128,2880]{0,1:T(8,128)(2,1)}), bf16[128,360]{0,1:T(8,128)(2,1)}) %reduce-scatter.9.cloned.1.call-update) | async-done | bytes 92176
  71.6 1.0 copy.64
  72.8 19.9 %all_gather.3 = bf16[128,2880]{0,1:T(8,128)(2,1)S(1)} all-gather(bf16[128,360]{0,1:T(8,128)(2,1)S(1)} %copy.66), channel_id=1, replica_groups=mesh['seq'=32,'tp'=8] {'tp'}, dimensions={1}, use_global_device_ids=true | all-gather | bytes 829440 | tf_op jit(solution)/shard_map/all_gather | solution.py:112
  93.6 6.5 %gather_fusion.1 = bf16[1024,2880]{1,0:T(8,128)(2,1)} fusion(bf16[129,2880]{1,0:T(8,128)(2,1)S(1)} %concatenate.25, s32[1024]{0:T(1024)S(1)} %fusion.58), kind=kCustom, calls=%fused_computation.1 | custom fusion | bytes 11800576 | tf_op jit(solution)/shard_map/gather | solution.py:132
  100.2 89.0 %all_to_all.15 = bf16[32,32,2880]{2,1,0:T(8,128)(2,1)S(1)} all-to-all(bf16[32,32,2880]{2,1,0:T(8,128)(2,1)} %bitcast.169), channel_id=1, replica_groups=mesh['seq'=32,'tp'=8] {'seq'}, dimensions={0} | all-to-all | bytes 11796480 | tf_op jit(solution)/shard_map/all_to_all | solution.py:133
  189.2 2.6 copy-done.2
  191.7 4.5 %fusion.6 = f32[32,32,360]{2,1,0:T(8,128)} fusion(bf16[32,32,2880]{2,1,0:T(8,128)(2,1)S(1)} %all_to_all.15, bf16[1,2880,360]{1,2,0:T(8,128)(2,1)S(1)} %copy-done.12), kind=kOutput, calls=%fused_computation.15 | convolution fusion | flops 2123366400 | bytes 9446400 | tf_op jit(solution)/shard_map/sexd,edf->sexf/dot_general | solution.py:135
  196.2 12.0 %convert_bitcast_fusion = bf16[32,1,32,2880]{3,2,0,1:T(8,128)(2,1)} fusion(bf16[1,360,2880]{2,1,0:T(8,128)(2,1)} %param.27, bf16[32,32,2880]{2,1,0:T(8,128)(2,1)} %copy-done.2, bf16[1,2880,360]{1,2,0:T(8,128)(2,1)} %param.26, f32[32,32,360]{2,1,0:T(8,128)} %fusion.6), kind=kOutput, calls=%fused_computation.4 | convolution fusion | flops 4252631040 | bytes 17418240 | tf_op jit(solution)/shard_map/sexf,efd->sexd/dot_general | solution.py:138
  208.2 32.1 %copy.80 = bf16[32,1,32,2880]{2,0,1,3:T(8,128)(2,1)} copy(bf16[32,1,32,2880]{3,2,0,1:T(8,128)(2,1)} %convert_bitcast_fusion) | data formatting | bytes 11796480
  240.3 32.1 %reshape.453 = bf16[2880,1024]{1,0:T(8,128)(2,1)} reshape(bf16[2880,1,32,32]{3,2,1,0:T(8,128)(2,1)} %bitcast.168) | data formatting | bytes 11796480
  272.5 66.5 %reduce-scatter.7.cloned.1.call-done = bf16[360,1024]{1,0:T(8,128)(2,1)} async-done(((bf16[2880,1024]{1,0:T(8,128)(2,1)}), bf16[360,1024]{1,0:T(8,128)(2,1)}) %reduce-scatter.7.cloned.1.call-update) | async-done | bytes 737296
  339.0 3.6 reshape.454
  342.6 4.5 %copy.81 = bf16[32,1,32,360]{3,2,0,1:T(8,128)(2,1)} copy(bf16[32,1,32,360]{2,0,1,3:T(8,128)(2,1)S(1)} %bitcast.170) | data formatting | bytes 1474560
  347.1 7.6 %all-to-all-start.2 = ((bf16[32,32,360]{2,1,0:T(8,128)(2,1)}), bf16[32,32,360]{2,1,0:T(8,128)(2,1)}, u32[]{:S(2)}, u32[]{:S(2)}) async-start(bf16[32,32,360]{2,1,0:T(8,128)(2,1)} %bitcast.171), calls=%async_computation.2 | async-start | bytes 1572864 | tf_op jit(solution)/shard_map/all_to_all | solution.py:140
  355.7 13.4 %all-to-all-done.2 = bf16[32,32,360]{2,1,0:T(8,128)(2,1)} async-done(((bf16[32,32,360]{2,1,0:T(8,128)(2,1)}), bf16[32,32,360]{2,1,0:T(8,128)(2,1)}, u32[]{:S(2)}, u32[]{:S(2)}) %all-to-all-start.2) | async-done | bytes 737312 | tf_op jit(solution)/shard_map/all_to_all | solution.py:140
  369.1 3.2 gather_fusion.2
  372.3 1.1 reshape.410
  373.4 1.7 multiply_reduce_fusion
  (75 shorter events, 7.2 us)
Async XLA Ops:
  7.2 26.4 %copy-start = (bf16[512,2880]{0,1:T(8,128)(2,1)S(1)}, bf16[512,2880]{0,1:T(8,128)(2,1)}, u32[]{:S(2)}) copy-start(bf16[512,2880]{0,1:T(8,128)(2,1)} %param.21) | copy-start | bytes 8847364
  10.4 18.7 %all-to-all-start = ((bf16[32,32,1,128]{3,1,2,0:T(8,128)(2,1)}), bf16[32,32,1,128]{3,1,2,0:T(8,128)(2,1)S(1)}, u32[]{:S(2)}, u32[]{:S(2)}) async-start(bf16[32,32,1,128]{3,1,2,0:T(8,128)(2,1)} %bitcast.5), calls=%async_computation | async-start | bytes 524288 | tf_op jit(solution)/shard_map/all_to_all | solution.py:67
  19.0 52.6 %reduce-scatter.9.cloned.1.call-start = ((), (), s32[]{:S(2)}) async-start(), calls=%async_computation.6 | async-start | bytes 829440
  29.1 1.8 copy-start.6
  29.1 1.8 copy-start.11
  29.1 1.9 copy-start.8
  29.1 1.8 copy-start.3
  32.0 1.2 copy-start.5
  33.5 1.9 copy-start.9
  33.6 2.2 copy-start.4
  35.4 58.0 %copy-start.7 = (f32[2880]{0:T(1024)S(1)}, f32[2880]{0:T(1024)}, u32[]{:S(2)}) copy-start(f32[2880]{0:T(1024)} %param.22) | copy-start | bytes 34564
  35.4 303.6 %reduce-scatter.7.cloned.1.call-start = ((), (), s32[]{:S(2)}) async-start(), calls=%async_computation.5 | async-start | bytes 6635520
  100.2 91.5 %copy-start.12 = (bf16[1,2880,360]{1,2,0:T(8,128)(2,1)S(1)}, bf16[1,2880,360]{1,2,0:T(8,128)(2,1)}, u32[]{:S(2)}) copy-start(bf16[1,2880,360]{1,2,0:T(8,128)(2,1)} %param.25) | copy-start | bytes 6220804
  189.2 2.6 copy-start.2
  342.6 12.2 %copy-start.10 = (f32[128,4]{0,1:T(4,128)S(1)}, f32[128,4]{0,1:T(4,128)}, u32[]{:S(2)}) copy-start(f32[128,4]{0,1:T(4,128)} %param.24) | copy-start | bytes 6148
  347.1 21.9 %all-to-all-start.2 = ((bf16[32,32,360]{2,1,0:T(8,128)(2,1)}), bf16[32,32,360]{2,1,0:T(8,128)(2,1)}, u32[]{:S(2)}, u32[]{:S(2)}) async-start(bf16[32,32,360]{2,1,0:T(8,128)(2,1)} %bitcast.171), calls=%async_computation.2 | async-start | bytes 1572864 | tf_op jit(solution)/shard_map/all_to_all | solution.py:140
  369.1 6.8 %copy-start.1 = (bf16[512,2880]{0,1:T(8,128)(2,1)S(1)}, bf16[512,2880]{0,1:T(8,128)(2,1)}, u32[]{:S(2)}) copy-start(bf16[512,2880]{0,1:T(8,128)(2,1)} %param.21) | copy-start | bytes 8847364
Sparse Core Ops, SparseCore 0:
  35.5 36.0 reduce-scatter.8
  272.6 66.3 reduce-scatter.6

commit v2 on v1

--- a/solution.py
+++ b/solution.py
@@ -135,8 +135,13 @@
     hidden = jnp.einsum("sexd,edf->sexf", arrived, w_gate, preferred_element_type=jnp.float32)
     lin = jnp.einsum("sexd,edf->sexf", arrived, w_up, preferred_element_type=jnp.float32)
     act = (hidden * jax.nn.sigmoid(1.702 * hidden) * (lin + 1.0)).astype(jnp.bfloat16)
-    down = jnp.einsum("sexf,efd->sexd", act, w_down, preferred_element_type=jnp.float32)
-    expert_out = lax.psum_scatter(down.astype(jnp.bfloat16), "tp", scatter_dimension=3, tiled=True)
+    tp_count = D // cols
+    w_down_split = w_down.reshape(local_e, w_down.shape[1], tp_count, cols)
+    down = jnp.einsum(
+        "sexf,efjk->jsexk", act, w_down_split, preferred_element_type=jnp.float32
+    ).astype(jnp.bfloat16)
+    down = down.reshape(tp_count * seq_count * local_e * cap, cols)
+    expert_out = lax.psum_scatter(down, "tp", scatter_dimension=0, tiled=True)
     returned = lax.all_to_all(
         expert_out.reshape(seq_count, local_e * cap, cols),
         "seq",

time: 384 us -> 339 us (0.88)
  blocking collectives: 109 us -> 22 us
  waiting for transfers between devices: 111 us -> 183 us
  local copies, waits for them, and re-layouts: 99.1 us -> 45 us
  starting transfers between devices: 16.3 us -> 34.9 us
    all_to_all x1 -> x0, blocking collectives: 89 us -> none  [per_device(): lax.all_to_all(outgoing_rows, 'seq', split_axis=0, concat_axis=0, tiled=T...]
    unnamed x36 -> x26, local copies, waits for them, and re-layouts: 77.7 us -> 2.75 us
    reduce_scatter x0 -> x1, waiting for transfers between devices: none -> 73.4 us  [per_device(): expert_out = lax.psum_scatter(down, 'tp', scatter_dimension=0, tiled=True)]
    unnamed x4 -> x3, waiting for transfers between devices: 98 us -> 31.7 us
    all_to_all x0 -> x1, waiting for transfers between devices: none -> 65 us  [per_device(): lax.all_to_all(outgoing_rows, 'seq', split_axis=0, concat_axis=0, tiled=T...]
    all_to_all x0 -> x1, starting transfers between devices: none -> 18.4 us  [per_device(): lax.all_to_all(outgoing_rows, 'seq', split_axis=0, concat_axis=0, tiled=T...]
    gather x1, local copies, waits for them, and re-layouts: 6.55 us -> 12.9 us  [per_device(): outgoing_rows = padded[source].reshape(seq_count, local_e * cap, D)]
    convert_element_type x0 -> x1, local copies, waits for them, and re-layouts: none -> 6.29 us  [per_device(): down = jnp.einsum('sexf,efjk->jsexk', act, w_down_split, preferred_elemen...]
  transfers between devices with their start and end apart: 4 -> 5, of which waited for: 3 -> 4; matrix products, arithmetic and copies ran while one was open for 4% -> 6% of each run, Pallas kernels for 0% -> 0%
where the time goes in v2:
time: 339 us; the launch traced here: 338 us
  waiting for transfers between devices  183 us (54%)
  local copies, waits for them, and re-layouts  45 us (13%)
  starting transfers between devices  34.9 us (10%)
  matrix products  27.3 us (8%)
  blocking collectives  22 us (6%)
  between operations  14.4 us (4%)
  other arithmetic  11 us (3%)
    reduce_scatter x1, waiting for transfers between devices, per_device(): expert_out = lax.psum_scatter(down, 'tp', scatter_dimension=0, tiled=True)  73.4 us
    all_to_all x1, waiting for transfers between devices, per_device(): lax.all_to_all(outgoing_rows, 'seq', split_axis=0, concat_axis=0, tiled=T...  65 us
    unnamed x3, waiting for transfers between devices  31.7 us
    all_gather x1, blocking collectives, per_device(): lax.all_gather(resid, 'tp', axis=1, tiled=True).astype(jnp.float32)  22 us
    all_to_all x1, starting transfers between devices, per_device(): lax.all_to_all(outgoing_rows, 'seq', split_axis=0, concat_axis=0, tiled=T...  18.4 us
    all_to_all x1, waiting for transfers between devices, per_device(): lax.all_to_all(expert_out.reshape(seq_count, local_e * cap, cols), 'seq',...  13.4 us
    gather x1, local copies, waits for them, and re-layouts, per_device(): outgoing_rows = padded[source].reshape(seq_count, local_e * cap, D)  12.9 us
    dot_general x1, matrix products, per_device(): jnp.einsum('sexf,efjk->jsexk', act, w_down_split, preferred_element_type=...  12.2 us
  transfers between devices with their start and end apart: 5, of which 4 were waited for; matrix products, arithmetic and copies ran while one was open for 6% of the time, Pallas kernels for 0%

profile of v2, /device:TPU:1, one launch (start us, length us, event | category | flops | bytes accessed | tf_op | source)
XLA Modules:
  0.0 338.2 jit_solution(8572872947774228253)
XLA Ops:
  7.2 1.0 add_select_fusion.1
  8.2 2.2 gather_fusion
  10.4 8.6 %all-to-all-start = ((bf16[32,32,1,128]{3,1,2,0:T(8,128)(2,1)}), bf16[32,32,1,128]{3,1,2,0:T(8,128)(2,1)S(1)}, u32[]{:S(2)}, u32[]{:S(2)}) async-start(bf16[32,32,1,128]{3,1,2,0:T(8,128)(2,1)} %bitcast.5), calls=%async_computation | async-start | bytes 524288 | tf_op jit(solution)/shard_map/all_to_all | solution.py:67
  19.1 1.2 dynamic_slice.7
  21.0 1.0 copy.61
  22.1 1.3 add_compare_fusion
  25.3 1.3 lt.56
  26.6 2.5 fusion.73
  29.3 1.6 bitcast_reduce_fusion
  32.0 1.1 fusion.10
  33.6 1.8 convolution_convert_fusion
  35.9 1.2 reduce-window.6
  37.7 2.4 scatter_custom_fusion
  40.1 31.7 %reduce-scatter.7.cloned.1.call-done = bf16[128,360]{0,1:T(8,128)(2,1)} async-done(((bf16[128,2880]{0,1:T(8,128)(2,1)}), bf16[128,360]{0,1:T(8,128)(2,1)}) %reduce-scatter.7.cloned.1.call-update) | async-done | bytes 92176
  71.8 1.0 copy.69
  73.0 22.0 %all_gather.3 = bf16[128,2880]{0,1:T(8,128)(2,1)} all-gather(bf16[128,360]{0,1:T(8,128)(2,1)S(1)} %copy.71), channel_id=1, replica_groups=mesh['seq'=32,'tp'=8] {'tp'}, dimensions={1}, use_global_device_ids=true | all-gather | bytes 829440 | tf_op jit(solution)/shard_map/all_gather | solution.py:112
  95.0 2.3 copy.72
  97.2 1.4 fusion.18
  98.6 1.4 fusion.20
  100.9 12.9 %gather_fusion.1 = bf16[1024,2880]{1,0:T(8,128)(2,1)} fusion(bf16[129,2880]{1,0:T(8,128)(2,1)} %concatenate.25, s32[1024]{0:T(1024)S(1)} %fusion.59), kind=kCustom, calls=%fused_computation.1 | custom fusion | bytes 11800576 | tf_op jit(solution)/shard_map/gather | solution.py:132
  113.8 18.4 %all-to-all-start.1 = ((bf16[32,32,2880]{2,1,0:T(8,128)(2,1)}), bf16[32,32,2880]{2,1,0:T(8,128)(2,1)}, u32[]{:S(2)}, u32[]{:S(2)}) async-start(bf16[32,32,2880]{2,1,0:T(8,128)(2,1)} %bitcast.167), calls=%async_computation.1 | async-start | bytes 12058624 | tf_op jit(solution)/shard_map/all_to_all | solution.py:133
  132.5 5.5 %reshape.411 = bf16[360,8,360]{2,1,0:T(8,128)(2,1)} reshape(bf16[1,360,2880]{2,1,0:T(8,128)(2,1)} %param.27) | data formatting | bytes 4147200 | tf_op jit(solution)/shard_map/reshape.43
  138.0 65.0 %all-to-all-done.1 = bf16[32,32,2880]{2,1,0:T(8,128)(2,1)} async-done(((bf16[32,32,2880]{2,1,0:T(8,128)(2,1)}), bf16[32,32,2880]{2,1,0:T(8,128)(2,1)}, u32[]{:S(2)}, u32[]{:S(2)}) %all-to-all-start.1) | async-done | bytes 5898272 | tf_op jit(solution)/shard_map/all_to_all | solution.py:133
  203.0 7.9 %fusion.7 = f32[32,32,360]{2,1,0:T(8,128)} fusion(bf16[32,32,2880]{2,1,0:T(8,128)(2,1)} %all-to-all-done.1, bf16[1,2880,360]{1,2,0:T(8,128)(2,1)} %param.25), kind=kOutput, calls=%fused_computation.16 | convolution fusion | flops 2123366400 | bytes 9446400 | tf_op jit(solution)/shard_map/sexd,edf->sexf/dot_general | solution.py:135
  210.9 12.2 %convert_bitcast_fusion = bf16[8,32,1,32,360]{4,3,0,1,2:T(8,128)(2,1)} fusion(bf16[360,8,360]{2,1,0:T(8,128)(2,1)} %reshape.411, bf16[32,32,2880]{2,1,0:T(8,128)(2,1)} %all-to-all-done.1, bf16[1,2880,360]{1,2,0:T(8,128)(2,1)} %param.26, f32[32,32,360]{2,1,0:T(8,128)} %fusion.7), kind=kOutput, calls=%fused_computation.4 | convolution fusion | flops 4252631040 | bytes 17418240 | tf_op jit(solution)/shard_map/sexf,efjk->jsexk/dot_general | solution.py:140
  223.1 6.3 %copy.78 = bf16[8,32,1,32,360]{4,3,1,0,2:T(8,128)(2,1)} copy(bf16[8,32,1,32,360]{4,3,0,1,2:T(8,128)(2,1)} %convert_bitcast_fusion) | data formatting | bytes 11796480 | tf_op jit(solution)/shard_map/convert_element_type | solution.py:142
  229.4 73.4 %reduce-scatter.5.cloned.1.call-done = bf16[1024,360]{1,0:T(8,128)(2,1)} async-done(((bf16[8192,360]{1,0:T(8,128)(2,1)}), bf16[1024,360]{1,0:T(8,128)(2,1)}) %reduce-scatter.5.cloned.1.call-update) | async-done | bytes 737296 | tf_op jit(solution)/shard_map/reduce_scatter | solution.py:144
  302.8 7.6 %all-to-all-start.2 = ((bf16[32,32,360]{2,1,0:T(8,128)(2,1)}), bf16[32,32,360]{2,1,0:T(8,128)(2,1)}, u32[]{:S(2)}, u32[]{:S(2)}) async-start(bf16[32,32,360]{2,1,0:T(8,128)(2,1)} %bitcast.170), calls=%async_computation.3 | async-start | bytes 1572864 | tf_op jit(solution)/shard_map/all_to_all | solution.py:145
  311.3 13.4 %all-to-all-done.2 = bf16[32,32,360]{2,1,0:T(8,128)(2,1)} async-done(((bf16[32,32,360]{2,1,0:T(8,128)(2,1)}), bf16[32,32,360]{2,1,0:T(8,128)(2,1)}, u32[]{:S(2)}, u32[]{:S(2)}) %all-to-all-start.2) | async-done | bytes 737312 | tf_op jit(solution)/shard_map/all_to_all | solution.py:145
  324.7 3.0 gather_fusion.2
  327.8 1.1 reshape.416
  328.8 1.7 multiply_reduce_fusion
  (68 shorter events, 8.4 us)
Async XLA Ops:
  7.2 26.4 %copy-start = (bf16[512,2880]{0,1:T(8,128)(2,1)S(1)}, bf16[512,2880]{0,1:T(8,128)(2,1)}, u32[]{:S(2)}) copy-start(bf16[512,2880]{0,1:T(8,128)(2,1)} %param.21) | copy-start | bytes 8847364
  10.4 18.7 %all-to-all-start = ((bf16[32,32,1,128]{3,1,2,0:T(8,128)(2,1)}), bf16[32,32,1,128]{3,1,2,0:T(8,128)(2,1)S(1)}, u32[]{:S(2)}, u32[]{:S(2)}) async-start(bf16[32,32,1,128]{3,1,2,0:T(8,128)(2,1)} %bitcast.5), calls=%async_computation | async-start | bytes 524288 | tf_op jit(solution)/shard_map/all_to_all | solution.py:67
  19.0 52.8 %reduce-scatter.7.cloned.1.call-start = ((), (), s32[]{:S(2)}) async-start(), calls=%async_computation.6 | async-start | bytes 829440
  29.1 1.8 copy-start.4
  29.1 1.8 copy-start.9
  29.1 1.9 copy-start.6
  29.1 1.8 copy-start.1
  32.0 1.2 copy-start.3
  33.5 1.9 copy-start.7
  33.5 2.2 copy-start.2
  35.4 63.3 %copy-start.5 = (f32[2880]{0:T(1024)S(1)}, f32[2880]{0:T(1024)}, u32[]{:S(2)}) copy-start(f32[2880]{0:T(1024)} %param.22) | copy-start | bytes 34564
  113.8 89.2 %all-to-all-start.1 = ((bf16[32,32,2880]{2,1,0:T(8,128)(2,1)}), bf16[32,32,2880]{2,1,0:T(8,128)(2,1)}, u32[]{:S(2)}, u32[]{:S(2)}) async-start(bf16[32,32,2880]{2,1,0:T(8,128)(2,1)} %bitcast.167), calls=%async_computation.1 | async-start | bytes 12058624 | tf_op jit(solution)/shard_map/all_to_all | solution.py:133
  132.3 170.5 %reduce-scatter.5.cloned.1.call-start = ((), (), s32[]{:S(2)}) async-start(), calls=%async_computation.5 | async-start | bytes 7077888 | tf_op jit(solution)/shard_map/reduce_scatter | solution.py:144
  229.3 81.1 %copy-start.8 = (f32[128,4]{0,1:T(4,128)S(1)}, f32[128,4]{0,1:T(4,128)}, u32[]{:S(2)}) copy-start(f32[128,4]{0,1:T(4,128)} %param.24) | copy-start | bytes 6148
  302.8 21.9 %all-to-all-start.2 = ((bf16[32,32,360]{2,1,0:T(8,128)(2,1)}), bf16[32,32,360]{2,1,0:T(8,128)(2,1)}, u32[]{:S(2)}, u32[]{:S(2)}) async-start(bf16[32,32,360]{2,1,0:T(8,128)(2,1)} %bitcast.170), calls=%async_computation.3 | async-start | bytes 1572864 | tf_op jit(solution)/shard_map/all_to_all | solution.py:145
Sparse Core Ops, SparseCore 0:
  35.5 36.2 reduce-scatter.6
  229.5 73.2 reduce-scatter.4

commit v3 on v1

--- a/solution.py
+++ b/solution.py
@@ -104,12 +104,15 @@
     attended = attended.transpose(2, 0, 1, 3).reshape(rows, local_q * head)
 
     partial_value = jnp.dot(attended, out_weight, preferred_element_type=jnp.float32)
-    column_sums = lax.psum_scatter(
-        partial_value.astype(jnp.bfloat16), "tp", scatter_dimension=1, tiled=True
-    ).astype(jnp.float32)
+    tp_count = D // cols
+    blocks = partial_value.astype(jnp.bfloat16).reshape(rows, tp_count, cols).transpose(1, 0, 2)
+    blocks = lax.all_to_all(blocks, "tp", split_axis=0, concat_axis=0, tiled=True)
+    column_sums = jnp.sum(blocks.astype(jnp.float32), 0)
     resid = (x_resid.astype(jnp.float32) + column_sums).astype(jnp.bfloat16)
     resid_wide = resid.astype(jnp.float32)
-    resid_full = lax.all_gather(resid, "tp", axis=1, tiled=True).astype(jnp.float32)
+    spread = jnp.broadcast_to(resid[None], (tp_count, rows, cols))
+    spread = lax.all_to_all(spread, "tp", split_axis=0, concat_axis=0, tiled=True)
+    resid_full = spread.transpose(1, 0, 2).reshape(rows, D).astype(jnp.float32)
     squares = jnp.sum(resid_full * resid_full, 1)
     scale_rows = lax.rsqrt(squares / D + norm_eps)
     normed_full = (resid_full * scale_rows[:, None] * norm_gain[None, :]).astype(jnp.bfloat16)
@@ -128,22 +131,35 @@
         .at[slot]
         .set(jnp.arange(rows * topk, dtype=jnp.int32) // topk)
     )
-    padded = jnp.concatenate([normed_full, jnp.zeros((1, D), jnp.bfloat16)], 0)
-    outgoing_rows = padded[source].reshape(seq_count, local_e * cap, D)
-    incoming_rows = lax.all_to_all(outgoing_rows, "seq", split_axis=0, concat_axis=0, tiled=True)
-    arrived = incoming_rows.reshape(seq_count, local_e, cap, D)
-    hidden = jnp.einsum("sexd,edf->sexf", arrived, w_gate, preferred_element_type=jnp.float32)
-    lin = jnp.einsum("sexd,edf->sexf", arrived, w_up, preferred_element_type=jnp.float32)
-    act = (hidden * jax.nn.sigmoid(1.702 * hidden) * (lin + 1.0)).astype(jnp.bfloat16)
-    down = jnp.einsum("sexf,efd->sexd", act, w_down, preferred_element_type=jnp.float32)
-    expert_out = lax.psum_scatter(down.astype(jnp.bfloat16), "tp", scatter_dimension=3, tiled=True)
-    returned = lax.all_to_all(
-        expert_out.reshape(seq_count, local_e * cap, cols),
-        "seq",
-        split_axis=0,
-        concat_axis=0,
-        tiled=True,
-    )
+    picks = (source[:, None] == jnp.arange(rows, dtype=jnp.int32)[None, :]).astype(jnp.bfloat16)
+    outgoing_rows = jnp.dot(picks, normed_full, preferred_element_type=jnp.float32).astype(
+        jnp.bfloat16
+    ).reshape(seq_count, local_e, cap, D)
+    w_down_split = w_down.reshape(local_e, w_down.shape[1], tp_count, cols)
+    chunks = 2
+    part = cap // chunks
+    pieces = []
+    for c in range(chunks):
+        sent = outgoing_rows[:, :, c * part:(c + 1) * part].reshape(seq_count, local_e * part, D)
+        arrived = lax.all_to_all(sent, "seq", split_axis=0, concat_axis=0, tiled=True)
+        arrived = arrived.reshape(seq_count, local_e, part, D)
+        hidden = jnp.einsum("sexd,edf->sexf", arrived, w_gate, preferred_element_type=jnp.float32)
+        lin = jnp.einsum("sexd,edf->sexf", arrived, w_up, preferred_element_type=jnp.float32)
+        act = (hidden * jax.nn.sigmoid(1.702 * hidden) * (lin + 1.0)).astype(jnp.bfloat16)
+        down = jnp.einsum(
+            "sexf,efjk->jsexk", act, w_down_split, preferred_element_type=jnp.float32
+        ).astype(jnp.bfloat16)
+        down = down.reshape(tp_count * seq_count * local_e * part, cols)
+        expert_out = lax.psum_scatter(down, "tp", scatter_dimension=0, tiled=True)
+        back = lax.all_to_all(
+            expert_out.reshape(seq_count, local_e * part, cols),
+            "seq",
+            split_axis=0,
+            concat_axis=0,
+            tiled=True,
+        )
+        pieces.append(back.reshape(seq_count, local_e, part, cols))
+    returned = jnp.concatenate(pieces, 2)
     taken = (
         returned.reshape(experts_all * cap, cols)[slot]
         .reshape(rows, topk, cols)

time: 384 us -> 313 us (0.82)
  local copies, waits for them, and re-layouts: 99.1 us -> 46.4 us
  blocking collectives: 109 us -> 74.8 us
  waiting for transfers between devices: 111 us -> 91.7 us
  starting transfers between devices: 16.3 us -> 34 us
  matrix products: 23.8 us -> 35.8 us
  other arithmetic: 8.8 us -> 14.1 us
    unnamed x4 -> x2, waiting for transfers between devices: 98 us -> 0.03 us
    unnamed x36 -> x30, local copies, waits for them, and re-layouts: 77.7 us -> 4.45 us
    all_to_all x1 -> x4, waiting for transfers between devices: 13.4 us -> 59 us  [the longest x1 32.7 us: per_device(): lax.all_to_all(sent, 'seq', split_axis=0, concat_axis=0, tiled=True)]
    reduce_scatter x0 -> x2, waiting for transfers between devices: none -> 32.6 us  [per_device(): expert_out = lax.psum_scatter(down, 'tp', scatter_dimension=0, tiled=True)]
    all_gather x1 -> x0, blocking collectives: 19.9 us -> none  [per_device(): lax.all_gather(resid, 'tp', axis=1, tiled=True).astype(jnp.float32)]
    all_to_all x1 -> x4, starting transfers between devices: 7.63 us -> 25.2 us  [the longest x2 14.6 us: per_device(): lax.all_to_all(expert_out.reshape(seq_count, local_e * part, cols), 'seq'...]
    convert_element_type x1 -> x3, local copies, waits for them, and re-layouts: 0.12 us -> 16.3 us  [the longest x1 8.5 us: per_device(): jnp.dot(picks, normed_full, preferred_element_type=jnp.float32)]
    all_to_all x1 -> x2, blocking collectives: 89 us -> 74.8 us  [the longest x1 44.4 us: per_device(): lax.all_to_all(sent, 'seq', split_axis=0, concat_axis=0, tiled=True)]
  transfers between devices with their start and end apart: 4 -> 7, of which waited for: 3 -> 4; matrix products, arithmetic and copies ran while one was open for 4% -> 12% of each run, Pallas kernels for 0% -> 0%
where the time goes in v3:
time: 313 us; the launch traced here: 311 us
  waiting for transfers between devices  91.7 us (29%)
  blocking collectives  74.8 us (24%)
  local copies, waits for them, and re-layouts  46.4 us (15%)
  matrix products  35.8 us (11%)
  starting transfers between devices  34 us (11%)
  between operations  14.4 us (5%)
  other arithmetic  14.1 us (5%)
    all_to_all x1, blocking collectives, per_device(): lax.all_to_all(sent, 'seq', split_axis=0, concat_axis=0, tiled=True)  44.4 us
    all_to_all x1, waiting for transfers between devices, per_device(): lax.all_to_all(sent, 'seq', split_axis=0, concat_axis=0, tiled=True)  32.7 us
    reduce_scatter x2, waiting for transfers between devices, per_device(): expert_out = lax.psum_scatter(down, 'tp', scatter_dimension=0, tiled=True)  32.6 us
    all_to_all x1, blocking collectives, per_device(): lax.all_to_all(blocks, 'tp', split_axis=0, concat_axis=0, tiled=True)  30.3 us
    all_to_all x1, waiting for transfers between devices, per_device(): lax.all_to_all(spread, 'tp', split_axis=0, concat_axis=0, tiled=True)  17.9 us
    dot_general x2, matrix products, per_device(): jnp.einsum('sexf,efjk->jsexk', act, w_down_split, preferred_element_type=...  17.3 us
    all_to_all x2, starting transfers between devices, per_device(): lax.all_to_all(expert_out.reshape(seq_count, local_e * part, cols), 'seq'...  14.6 us
    all_to_all x1, starting transfers between devices, per_device(): lax.all_to_all(outgoing, 'seq', split_axis=0, concat_axis=0, tiled=True)  8.57 us
  transfers between devices with their start and end apart: 7, of which 4 were waited for; matrix products, arithmetic and copies ran while one was open for 12% of the time, Pallas kernels for 0%

profile of v3, /device:TPU:1, one launch (start us, length us, event | category | flops | bytes accessed | tf_op | source)
XLA Modules:
  0.0 311.1 jit_solution(9683853843067001976)
XLA Ops:
  8.2 2.2 gather_fusion
  10.4 8.6 %all-to-all-start = ((bf16[32,32,1,128]{3,1,2,0:T(8,128)(2,1)}), bf16[32,32,1,128]{3,1,2,0:T(8,128)(2,1)S(1)}, u32[]{:S(2)}, u32[]{:S(2)}) async-start(bf16[32,32,1,128]{3,1,2,0:T(8,128)(2,1)} %bitcast.5), calls=%async_computation | async-start | bytes 524288 | tf_op jit(solution)/shard_map/all_to_all | solution.py:67
  26.6 2.5 fusion.114
  29.2 1.6 bitcast_reduce_fusion
  34.5 30.3 %all_to_all.35 = bf16[8,128,360]{1,2,0:T(8,128)(2,1)S(1)} all-to-all(bf16[8,128,360]{1,2,0:T(8,128)(2,1)S(1)} %bitcast.238), channel_id=1, replica_groups=mesh['seq'=32,'tp'=8] {'tp'}, dimensions={0} | all-to-all | bytes 1474560 | tf_op jit(solution)/shard_map/all_to_all | solution.py:109
  65.9 4.2 %all-to-all-start.2 = ((bf16[8,128,360]{1,2,0:T(8,128)(2,1)}), bf16[8,128,360]{1,2,0:T(8,128)(2,1)}, u32[]{:S(2)}, u32[]{:S(2)}) async-start(bf16[8,128,360]{1,2,0:T(8,128)(2,1)} %broadcast_in_dim.49), calls=%async_computation.2 | async-start | bytes 1474560 | tf_op jit(solution)/shard_map/all_to_all | solution.py:114
  72.3 2.4 scatter_custom_fusion
  74.7 17.9 %all-to-all-done.2 = bf16[8,128,360]{1,2,0:T(8,128)(2,1)} async-done(((bf16[8,128,360]{1,2,0:T(8,128)(2,1)}), bf16[8,128,360]{1,2,0:T(8,128)(2,1)}, u32[]{:S(2)}, u32[]{:S(2)}) %all-to-all-start.2) | async-done | bytes 737312 | tf_op jit(solution)/shard_map/all_to_all | solution.py:114
  92.6 1.5 multiply_reduce_fusion
  94.1 1.6 fusion.20
  95.7 4.4 %convolution_convert_fusion = bf16[1024,2880]{0,1:T(8,128)(2,1)} fusion(bf16[128,2880]{0,1:T(8,128)(2,1)S(1)} %fusion.20, s32[1024]{0:T(1024)S(1)} %scatter_custom_fusion), kind=kOutput, calls=%fused_computation.3 | convolution fusion | flops 758054912 | bytes 6639616 | tf_op jit(solution)/shard_map/dot_general | solution.py:135
  100.1 8.5 %copy.81 = bf16[1024,2880]{1,0:T(8,128)(2,1)} copy(bf16[1024,2880]{0,1:T(8,128)(2,1)} %convolution_convert_fusion) | data formatting | bytes 11796480 | tf_op jit(solution)/shard_map/convert_element_type | solution.py:135
  108.6 5.8 %slice_bitcast_fusion.1 = (bf16[32,16,2880]{2,1,0:T(8,128)(2,1)}, bf16[32,16,2880]{2,1,0:T(8,128)(2,1)}) fusion(bf16[32,1,32,2880]{3,2,0,1:T(8,128)(2,1)} %bitcast.234), kind=kLoop, calls=%fused_computation.14 | loop fusion | bytes 11796480 | tf_op jit(solution)/shard_map/reshape | solution.py:143
  114.3 6.4 %all-to-all-start.3 = ((bf16[32,16,2880]{2,1,0:T(8,128)(2,1)}), bf16[32,16,2880]{2,1,0:T(8,128)(2,1)}, u32[]{:S(2)}, u32[]{:S(2)}) async-start(bf16[32,16,2880]{2,1,0:T(8,128)(2,1)} %get-tuple-element.10), calls=%async_computation.3 | async-start | bytes 6029312 | tf_op jit(solution)/shard_map/all_to_all | solution.py:144
  121.0 5.5 %reshape.457 = bf16[360,8,360]{2,1,0:T(8,128)(2,1)} reshape(bf16[1,360,2880]{2,1,0:T(8,128)(2,1)} %param.27) | data formatting | bytes 4147200 | tf_op jit(solution)/shard_map/reshape.52
  126.5 32.7 %all-to-all-done.3 = bf16[32,16,2880]{2,1,0:T(8,128)(2,1)} async-done(((bf16[32,16,2880]{2,1,0:T(8,128)(2,1)}), bf16[32,16,2880]{2,1,0:T(8,128)(2,1)}, u32[]{:S(2)}, u32[]{:S(2)}) %all-to-all-start.3) | async-done | bytes 2949152 | tf_op jit(solution)/shard_map/all_to_all | solution.py:144
  159.2 5.1 %fusion.21 = f32[32,1,16,360]{3,2,0,1:T(8,128)} fusion(bf16[32,16,2880]{2,1,0:T(8,128)(2,1)} %all-to-all-done.3, bf16[1,2880,360]{1,2,0:T(8,128)(2,1)} %param.25), kind=kOutput, calls=%fused_computation.35 | convolution fusion | flops 1061683200 | bytes 5760000 | tf_op jit(solution)/shard_map/sexd,edf->sexf/dot_general | solution.py:146
  164.4 8.6 %convert_bitcast_fusion.1 = bf16[8,32,1,16,360]{4,3,0,1,2:T(8,128)(2,1)} fusion(bf16[360,8,360]{2,1,0:T(8,128)(2,1)} %reshape.457, bf16[32,16,2880]{2,1,0:T(8,128)(2,1)} %all-to-all-done.3, bf16[1,2880,360]{1,2,0:T(8,128)(2,1)} %param.26, f32[32,1,16,360]{3,2,0,1:T(8,128)} %fusion.21), kind=kOutput, calls=%fused_computation.12 | convolution fusion | flops 2126315520 | bytes 10782720 | tf_op jit(solution)/shard_map/sexf,efjk->jsexk/dot_general | solution.py:149
  173.0 3.9 %copy.83 = bf16[8,32,1,16,360]{4,3,1,0,2:T(8,128)(2,1)} copy(bf16[8,32,1,16,360]{4,3,0,1,2:T(8,128)(2,1)} %convert_bitcast_fusion.1) | data formatting | bytes 5898240 | tf_op jit(solution)/shard_map/convert_element_type | solution.py:151
  177.0 44.4 %all_to_all.36 = bf16[32,16,2880]{2,1,0:T(8,128)(2,1)S(1)} all-to-all(bf16[32,16,2880]{2,1,0:T(8,128)(2,1)} %get-tuple-element.11), channel_id=1, replica_groups=mesh['seq'=32,'tp'=8] {'seq'}, dimensions={0} | all-to-all | bytes 5898240 | tf_op jit(solution)/shard_map/all_to_all | solution.py:144
  221.4 1.7 copy-done.1
  223.0 2.6 fusion.24
  225.7 8.6 %convert_bitcast_fusion = bf16[8,32,1,16,360]{4,3,0,1,2:T(8,128)(2,1)} fusion(bf16[360,8,360]{2,1,0:T(8,128)(2,1)} %reshape.457, bf16[32,16,2880]{2,1,0:T(8,128)(2,1)} %copy-done.1, bf16[1,2880,360]{1,2,0:T(8,128)(2,1)} %param.26, f32[32,1,16,360]{3,2,0,1:T(8,128)} %fusion.24), kind=kOutput, calls=%fused_computation.11 | convolution fusion | flops 2126315520 | bytes 10782720 | tf_op jit(solution)/shard_map/sexf,efjk->jsexk/dot_general | solution.py:149
  234.3 3.9 %copy.85 = bf16[8,32,1,16,360]{4,3,1,0,2:T(8,128)(2,1)} copy(bf16[8,32,1,16,360]{4,3,0,1,2:T(8,128)(2,1)} %convert_bitcast_fusion) | data formatting | bytes 5898240 | tf_op jit(solution)/shard_map/convert_element_type | solution.py:151
  238.3 4.0 %all-to-all-start.4 = ((bf16[32,16,360]{2,1,0:T(8,128)(2,1)}), bf16[32,16,360]{2,1,0:T(8,128)(2,1)S(1)}, u32[]{:S(2)}, u32[]{:S(2)}) async-start(bf16[32,16,360]{2,1,0:T(8,128)(2,1)} %bitcast.244), calls=%async_computation.5 | async-start | bytes 786432 | tf_op jit(solution)/shard_map/all_to_all | solution.py:154
  242.3 32.6 %reduce-scatter.5.cloned.1.call-done = bf16[512,360]{1,0:T(8,128)(2,1)} async-done(((bf16[4096,360]{1,0:T(8,128)(2,1)}), bf16[512,360]{1,0:T(8,128)(2,1)}) %reduce-scatter.5.cloned.1.call-update) | async-done | bytes 368656 | tf_op jit(solution)/shard_map/reduce_scatter | solution.py:153
  274.8 10.6 %all-to-all-start.6 = ((bf16[32,16,360]{2,1,0:T(8,128)(2,1)}), bf16[32,16,360]{2,1,0:T(8,128)(2,1)}, u32[]{:S(2)}, u32[]{:S(2)}) async-start(bf16[32,16,360]{2,1,0:T(8,128)(2,1)} %bitcast.245), calls=%async_computation.8 | async-start | bytes 786432 | tf_op jit(solution)/shard_map/all_to_all | solution.py:154
  285.6 1.7 copy.87
  287.3 8.4 %all-to-all-done.6 = bf16[32,16,360]{2,1,0:T(8,128)(2,1)} async-done(((bf16[32,16,360]{2,1,0:T(8,128)(2,1)}), bf16[32,16,360]{2,1,0:T(8,128)(2,1)}, u32[]{:S(2)}, u32[]{:S(2)}) %all-to-all-start.6) | async-done | bytes 368672 | tf_op jit(solution)/shard_map/all_to_all | solution.py:154
  295.7 2.0 pad_maximum_fusion
  297.6 3.0 gather_fusion.1
  301.8 1.7 multiply_reduce_fusion.1
  (81 shorter events, 17.7 us)
Async XLA Ops:
  7.2 26.3 %copy-start = (bf16[512,2880]{0,1:T(8,128)(2,1)S(1)}, bf16[512,2880]{0,1:T(8,128)(2,1)}, u32[]{:S(2)}) copy-start(bf16[512,2880]{0,1:T(8,128)(2,1)} %param.21) | copy-start | bytes 8847364
  10.4 18.6 %all-to-all-start = ((bf16[32,32,1,128]{3,1,2,0:T(8,128)(2,1)}), bf16[32,32,1,128]{3,1,2,0:T(8,128)(2,1)S(1)}, u32[]{:S(2)}, u32[]{:S(2)}) async-start(bf16[32,32,1,128]{3,1,2,0:T(8,128)(2,1)} %bitcast.5), calls=%async_computation | async-start | bytes 524288 | tf_op jit(solution)/shard_map/all_to_all | solution.py:67
  29.1 1.8 copy-start.6
  29.1 1.8 copy-start.11
  29.1 1.9 copy-start.8
  29.1 1.8 copy-start.2
  31.9 1.2 copy-start.5
  33.5 1.0 copy-start.3
  33.5 31.4 %copy-start.4 = (bf16[128,360]{0,1:T(8,128)(2,1)S(1)}, bf16[128,360]{0,1:T(8,128)(2,1)}, u32[]{:S(2)}) copy-start(bf16[128,360]{0,1:T(8,128)(2,1)} %param.14) | copy-start | bytes 276484
  34.4 35.7 %copy-start.9 = (s32[128,4]{0,1:T(4,128)S(1)}, s32[128,4]{0,1:T(4,128)}, u32[]{:S(2)}) copy-start(s32[128,4]{0,1:T(4,128)} %param.23) | copy-start | bytes 6148
  34.5 59.7 %copy-start.7 = (f32[2880]{0:T(1024)S(1)}, f32[2880]{0:T(1024)}, u32[]{:S(2)}) copy-start(f32[2880]{0:T(1024)} %param.22) | copy-start | bytes 34564
  65.9 26.7 %all-to-all-start.2 = ((bf16[8,128,360]{1,2,0:T(8,128)(2,1)}), bf16[8,128,360]{1,2,0:T(8,128)(2,1)}, u32[]{:S(2)}, u32[]{:S(2)}) async-start(bf16[8,128,360]{1,2,0:T(8,128)(2,1)} %broadcast_in_dim.49), calls=%async_computation.2 | async-start | bytes 1474560 | tf_op jit(solution)/shard_map/all_to_all | solution.py:114
  114.3 44.9 %all-to-all-start.3 = ((bf16[32,16,2880]{2,1,0:T(8,128)(2,1)}), bf16[32,16,2880]{2,1,0:T(8,128)(2,1)}, u32[]{:S(2)}, u32[]{:S(2)}) async-start(bf16[32,16,2880]{2,1,0:T(8,128)(2,1)} %get-tuple-element.10), calls=%async_computation.3 | async-start | bytes 6029312 | tf_op jit(solution)/shard_map/all_to_all | solution.py:144
  120.7 117.5 %reduce-scatter.3.cloned.1.call-start = ((), (), s32[]{:S(2)}) async-start(), calls=%async_computation.9 | async-start | bytes 3538944 | tf_op jit(solution)/shard_map/reduce_scatter | solution.py:153
  176.9 97.9 %reduce-scatter.5.cloned.1.call-start = ((), (), s32[]{:S(2)}) async-start(), calls=%async_computation.10 | async-start | bytes 3538944 | tf_op jit(solution)/shard_map/reduce_scatter | solution.py:153
  176.9 46.1 %copy-start.12 = (bf16[1,2880,360]{1,2,0:T(8,128)(2,1)S(1)}, bf16[1,2880,360]{1,2,0:T(8,128)(2,1)}, u32[]{:S(2)}) copy-start(bf16[1,2880,360]{1,2,0:T(8,128)(2,1)} %param.25) | copy-start | bytes 6220804
  221.4 1.7 copy-start.1
  238.2 47.2 %copy-start.10 = (f32[128,4]{0,1:T(4,128)S(1)}, f32[128,4]{0,1:T(4,128)}, u32[]{:S(2)}) copy-start(f32[128,4]{0,1:T(4,128)} %param.24) | copy-start | bytes 6148
  238.3 36.6 %all-to-all-start.4 = ((bf16[32,16,360]{2,1,0:T(8,128)(2,1)}), bf16[32,16,360]{2,1,0:T(8,128)(2,1)S(1)}, u32[]{:S(2)}, u32[]{:S(2)}) async-start(bf16[32,16,360]{2,1,0:T(8,128)(2,1)} %bitcast.244), calls=%async_computation.5 | async-start | bytes 786432 | tf_op jit(solution)/shard_map/all_to_all | solution.py:154
  274.8 20.8 %all-to-all-start.6 = ((bf16[32,16,360]{2,1,0:T(8,128)(2,1)}), bf16[32,16,360]{2,1,0:T(8,128)(2,1)}, u32[]{:S(2)}, u32[]{:S(2)}) async-start(bf16[32,16,360]{2,1,0:T(8,128)(2,1)} %bitcast.245), calls=%async_computation.8 | async-start | bytes 786432 | tf_op jit(solution)/shard_map/all_to_all | solution.py:154
Sparse Core Ops, SparseCore 0:
  177.0 37.3 reduce-scatter.2
  238.4 36.4 reduce-scatter.4

commit v4 on v3

--- a/solution.py
+++ b/solution.py
@@ -106,8 +106,9 @@
     partial_value = jnp.dot(attended, out_weight, preferred_element_type=jnp.float32)
     tp_count = D // cols
     blocks = partial_value.astype(jnp.bfloat16).reshape(rows, tp_count, cols).transpose(1, 0, 2)
-    blocks = lax.all_to_all(blocks, "tp", split_axis=0, concat_axis=0, tiled=True)
-    column_sums = jnp.sum(blocks.astype(jnp.float32), 0)
+    column_sums = lax.psum_scatter(
+        blocks.reshape(tp_count * rows, cols), "tp", scatter_dimension=0, tiled=True
+    ).astype(jnp.float32)
     resid = (x_resid.astype(jnp.float32) + column_sums).astype(jnp.bfloat16)
     resid_wide = resid.astype(jnp.float32)
     spread = jnp.broadcast_to(resid[None], (tp_count, rows, cols))

time: 313 us -> 324 us (1.035)
  blocking collectives: 74.8 us -> 44.4 us
  waiting for transfers between devices: 91.7 us -> 122 us
  starting transfers between devices: 34 us -> 41 us
    reduce_scatter x0 -> x1, waiting for transfers between devices: none -> 36 us  [per_device(): lax.psum_scatter(blocks.reshape(tp_count * rows, cols), 'tp', scatter_dim...]
    all_to_all x1 -> x0, blocking collectives: 30.3 us -> none  [per_device(): lax.all_to_all(blocks, 'tp', split_axis=0, concat_axis=0, tiled=True)]
    all_to_all x1, starting transfers between devices: 6.37 us -> 13 us  [per_device(): lax.all_to_all(sent, 'seq', split_axis=0, concat_axis=0, tiled=True)]
    all_to_all x1, waiting for transfers between devices: 17.9 us -> 12.5 us  [per_device(): lax.all_to_all(spread, 'tp', split_axis=0, concat_axis=0, tiled=True)]
    unnamed x30 -> x33, local copies, waits for them, and re-layouts: 4.45 us -> 7.61 us
  transfers between devices with their start and end apart: 7 -> 8, of which waited for: 4 -> 5; matrix products, arithmetic and copies ran while one was open for 12% -> 12% of each run, Pallas kernels for 0% -> 0%
where the time goes in v4:
time: 324 us; the launch traced here: 322 us
  waiting for transfers between devices  122 us (38%)
  local copies, waits for them, and re-layouts  49.5 us (15%)
  blocking collectives  44.4 us (14%)
  starting transfers between devices  41 us (13%)
  matrix products  36.7 us (11%)
  other arithmetic  14.2 us (4%)
  between operations  14.1 us (4%)
    all_to_all x1, blocking collectives, per_device(): lax.all_to_all(sent, 'seq', split_axis=0, concat_axis=0, tiled=True)  44.4 us
    reduce_scatter x1, waiting for transfers between devices, per_device(): lax.psum_scatter(blocks.reshape(tp_count * rows, cols), 'tp', scatter_dim...  36 us
    all_to_all x1, waiting for transfers between devices, per_device(): lax.all_to_all(sent, 'seq', split_axis=0, concat_axis=0, tiled=True)  32.7 us
    reduce_scatter x2, waiting for transfers between devices, per_device(): expert_out = lax.psum_scatter(down, 'tp', scatter_dimension=0, tiled=True)  32.4 us
    dot_general x2, matrix products, per_device(): jnp.einsum('sexf,efjk->jsexk', act, w_down_split, preferred_element_type=...  17.3 us
    all_to_all x2, starting transfers between devices, per_device(): lax.all_to_all(expert_out.reshape(seq_count, local_e * part, cols), 'seq'...  14.7 us
    all_to_all x1, starting transfers between devices, per_device(): lax.all_to_all(sent, 'seq', split_axis=0, concat_axis=0, tiled=True)  13 us
    all_to_all x1, waiting for transfers between devices, per_device(): lax.all_to_all(spread, 'tp', split_axis=0, concat_axis=0, tiled=True)  12.5 us
  transfers between devices with their start and end apart: 8, of which 5 were waited for; matrix products, arithmetic and copies ran while one was open for 12% of the time, Pallas kernels for 0%

profile of v4, /device:TPU:1, one launch (start us, length us, event | category | flops | bytes accessed | tf_op | source)
XLA Modules:
  0.0 322.1 jit_solution(14535844913493454821)
XLA Ops:
  8.2 2.2 gather_fusion
  10.4 8.6 %all-to-all-start = ((bf16[32,32,1,128]{3,1,2,0:T(8,128)(2,1)}), bf16[32,32,1,128]{3,1,2,0:T(8,128)(2,1)S(1)}, u32[]{:S(2)}, u32[]{:S(2)}) async-start(bf16[32,32,1,128]{3,1,2,0:T(8,128)(2,1)} %bitcast.5), calls=%async_computation | async-start | bytes 524288 | tf_op jit(solution)/shard_map/all_to_all | solution.py:67
  26.7 2.5 fusion.114
  29.3 1.6 bitcast_reduce_fusion
  33.6 1.8 convolution_convert_fusion.1
  35.4 2.3 copy.83
  37.8 36.0 %reduce-scatter.10.cloned.1.call-done = bf16[128,360]{1,0:T(8,128)(2,1)} async-done(((bf16[1024,360]{1,0:T(8,128)(2,1)}), bf16[128,360]{1,0:T(8,128)(2,1)}) %reduce-scatter.10.cloned.1.call-update) | async-done | bytes 92176 | tf_op jit(solution)/shard_map/reduce_scatter | solution.py:109
  75.9 4.5 %all-to-all-start.1 = ((bf16[8,128,360]{1,2,0:T(8,128)(2,1)}), bf16[8,128,360]{1,2,0:T(8,128)(2,1)}, u32[]{:S(2)}, u32[]{:S(2)}) async-start(bf16[8,128,360]{1,2,0:T(8,128)(2,1)} %broadcast_in_dim.49), calls=%async_computation.1 | async-start | bytes 1474560 | tf_op jit(solution)/shard_map/all_to_all | solution.py:115
  82.5 2.4 scatter_custom_fusion
  84.9 12.5 %all-to-all-done.1 = bf16[8,128,360]{1,2,0:T(8,128)(2,1)} async-done(((bf16[8,128,360]{1,2,0:T(8,128)(2,1)}), bf16[8,128,360]{1,2,0:T(8,128)(2,1)}, u32[]{:S(2)}, u32[]{:S(2)}) %all-to-all-start.1) | async-done | bytes 737312 | tf_op jit(solution)/shard_map/all_to_all | solution.py:115
  100.5 4.4 %convolution_convert_fusion = bf16[1024,2880]{0,1:T(8,128)(2,1)} fusion(bf16[128,2880]{0,1:T(8,128)(2,1)S(1)} %fusion.20, s32[1024]{0:T(1024)S(1)} %scatter_custom_fusion), kind=kOutput, calls=%fused_computation.3 | convolution fusion | flops 758054912 | bytes 6639616 | tf_op jit(solution)/shard_map/dot_general | solution.py:136
  104.9 8.5 %copy.66 = bf16[1024,2880]{1,0:T(8,128)(2,1)} copy(bf16[1024,2880]{0,1:T(8,128)(2,1)} %convolution_convert_fusion) | data formatting | bytes 11796480 | tf_op jit(solution)/shard_map/convert_element_type | solution.py:136
  113.4 5.8 %slice_bitcast_fusion.1 = (bf16[32,16,2880]{2,1,0:T(8,128)(2,1)}, bf16[32,16,2880]{2,1,0:T(8,128)(2,1)}) fusion(bf16[32,1,32,2880]{3,2,0,1:T(8,128)(2,1)} %bitcast.236), kind=kLoop, calls=%fused_computation.14 | loop fusion | bytes 11796480 | tf_op jit(solution)/shard_map/reshape | solution.py:144
  119.2 13.0 %all-to-all-start.2 = ((bf16[32,16,2880]{2,1,0:T(8,128)(2,1)}), bf16[32,16,2880]{2,1,0:T(8,128)(2,1)}, u32[]{:S(2)}, u32[]{:S(2)}) async-start(bf16[32,16,2880]{2,1,0:T(8,128)(2,1)} %get-tuple-element.8), calls=%async_computation.2 | async-start | bytes 6029312 | tf_op jit(solution)/shard_map/all_to_all | solution.py:145
  132.4 5.5 %reshape.461 = bf16[360,8,360]{2,1,0:T(8,128)(2,1)} reshape(bf16[1,360,2880]{2,1,0:T(8,128)(2,1)} %param.27) | data formatting | bytes 4147200 | tf_op jit(solution)/shard_map/reshape.53
  137.9 32.7 %all-to-all-done.2 = bf16[32,16,2880]{2,1,0:T(8,128)(2,1)} async-done(((bf16[32,16,2880]{2,1,0:T(8,128)(2,1)}), bf16[32,16,2880]{2,1,0:T(8,128)(2,1)}, u32[]{:S(2)}, u32[]{:S(2)}) %all-to-all-start.2) | async-done | bytes 2949152 | tf_op jit(solution)/shard_map/all_to_all | solution.py:145
  170.6 5.1 %fusion.21 = f32[32,1,16,360]{3,2,0,1:T(8,128)} fusion(bf16[32,16,2880]{2,1,0:T(8,128)(2,1)} %all-to-all-done.2, bf16[1,2880,360]{1,2,0:T(8,128)(2,1)} %param.25), kind=kOutput, calls=%fused_computation.34 | convolution fusion | flops 1061683200 | bytes 5760000 | tf_op jit(solution)/shard_map/sexd,edf->sexf/dot_general | solution.py:147
  175.8 8.6 %convert_bitcast_fusion.1 = bf16[8,32,1,16,360]{4,3,0,1,2:T(8,128)(2,1)} fusion(bf16[360,8,360]{2,1,0:T(8,128)(2,1)} %reshape.461, bf16[32,16,2880]{2,1,0:T(8,128)(2,1)} %all-to-all-done.2, bf16[1,2880,360]{1,2,0:T(8,128)(2,1)} %param.26, f32[32,1,16,360]{3,2,0,1:T(8,128)} %fusion.21), kind=kOutput, calls=%fused_computation.12 | convolution fusion | flops 2126315520 | bytes 10782720 | tf_op jit(solution)/shard_map/sexf,efjk->jsexk/dot_general | solution.py:150
  184.4 3.9 %copy.68 = bf16[8,32,1,16,360]{4,3,1,0,2:T(8,128)(2,1)} copy(bf16[8,32,1,16,360]{4,3,0,1,2:T(8,128)(2,1)} %convert_bitcast_fusion.1) | data formatting | bytes 5898240 | tf_op jit(solution)/shard_map/convert_element_type | solution.py:152
  188.4 44.4 %all_to_all.30 = bf16[32,16,2880]{2,1,0:T(8,128)(2,1)S(1)} all-to-all(bf16[32,16,2880]{2,1,0:T(8,128)(2,1)} %get-tuple-element.9), channel_id=1, replica_groups=mesh['seq'=32,'tp'=8] {'seq'}, dimensions={0} | all-to-all | bytes 5898240 | tf_op jit(solution)/shard_map/all_to_all | solution.py:145
  232.8 1.7 copy-done.1
  234.4 2.6 fusion.24
  237.1 8.6 %convert_bitcast_fusion = bf16[8,32,1,16,360]{4,3,0,1,2:T(8,128)(2,1)} fusion(bf16[360,8,360]{2,1,0:T(8,128)(2,1)} %reshape.461, bf16[32,16,2880]{2,1,0:T(8,128)(2,1)} %copy-done.1, bf16[1,2880,360]{1,2,0:T(8,128)(2,1)} %param.26, f32[32,1,16,360]{3,2,0,1:T(8,128)} %fusion.24), kind=kOutput, calls=%fused_computation.11 | convolution fusion | flops 2126315520 | bytes 10782720 | tf_op jit(solution)/shard_map/sexf,efjk->jsexk/dot_general | solution.py:150
  245.7 3.9 %copy.70 = bf16[8,32,1,16,360]{4,3,1,0,2:T(8,128)(2,1)} copy(bf16[8,32,1,16,360]{4,3,0,1,2:T(8,128)(2,1)} %convert_bitcast_fusion) | data formatting | bytes 5898240 | tf_op jit(solution)/shard_map/convert_element_type | solution.py:152
  249.7 4.0 %all-to-all-start.3 = ((bf16[32,16,360]{2,1,0:T(8,128)(2,1)}), bf16[32,16,360]{2,1,0:T(8,128)(2,1)S(1)}, u32[]{:S(2)}, u32[]{:S(2)}) async-start(bf16[32,16,360]{2,1,0:T(8,128)(2,1)} %bitcast.247), calls=%async_computation.4 | async-start | bytes 786432 | tf_op jit(solution)/shard_map/all_to_all | solution.py:155
  253.7 32.4 %reduce-scatter.8.cloned.1.call-done = bf16[512,360]{1,0:T(8,128)(2,1)} async-done(((bf16[4096,360]{1,0:T(8,128)(2,1)}), bf16[512,360]{1,0:T(8,128)(2,1)}) %reduce-scatter.8.cloned.1.call-update) | async-done | bytes 368656 | tf_op jit(solution)/shard_map/reduce_scatter | solution.py:154
  286.0 10.8 %all-to-all-start.5 = ((bf16[32,16,360]{2,1,0:T(8,128)(2,1)}), bf16[32,16,360]{2,1,0:T(8,128)(2,1)}, u32[]{:S(2)}, u32[]{:S(2)}) async-start(bf16[32,16,360]{2,1,0:T(8,128)(2,1)} %bitcast.248), calls=%async_computation.7 | async-start | bytes 786432 | tf_op jit(solution)/shard_map/all_to_all | solution.py:155
  296.9 1.7 copy.71
  298.6 8.4 %all-to-all-done.5 = bf16[32,16,360]{2,1,0:T(8,128)(2,1)} async-done(((bf16[32,16,360]{2,1,0:T(8,128)(2,1)}), bf16[32,16,360]{2,1,0:T(8,128)(2,1)}, u32[]{:S(2)}, u32[]{:S(2)}) %all-to-all-start.5) | async-done | bytes 368672 | tf_op jit(solution)/shard_map/all_to_all | solution.py:155
  307.0 2.0 pad_maximum_fusion
  309.0 3.0 gather_fusion.1
  313.1 1.7 multiply_reduce_fusion.1
  (85 shorter events, 21.0 us)
Async XLA Ops:
  7.2 26.4 %copy-start = (bf16[512,2880]{0,1:T(8,128)(2,1)S(1)}, bf16[512,2880]{0,1:T(8,128)(2,1)}, u32[]{:S(2)}) copy-start(bf16[512,2880]{0,1:T(8,128)(2,1)} %param.21) | copy-start | bytes 8847364
  10.4 18.7 %all-to-all-start = ((bf16[32,32,1,128]{3,1,2,0:T(8,128)(2,1)}), bf16[32,32,1,128]{3,1,2,0:T(8,128)(2,1)S(1)}, u32[]{:S(2)}, u32[]{:S(2)}) async-start(bf16[32,32,1,128]{3,1,2,0:T(8,128)(2,1)} %bitcast.5), calls=%async_computation | async-start | bytes 524288 | tf_op jit(solution)/shard_map/all_to_all | solution.py:67
  19.0 54.8 %reduce-scatter.10.cloned.1.call-start = ((), (), s32[]{:S(2)}) async-start(), calls=%async_computation.11 | async-start | bytes 884736 | tf_op jit(solution)/shard_map/reduce_scatter | solution.py:109
  29.1 1.8 copy-start.6
  29.1 1.8 copy-start.11
  29.1 1.9 copy-start.8
  29.1 1.8 copy-start.2
  32.0 1.2 copy-start.5
  33.5 1.9 copy-start.3
  33.5 4.2 %copy-start.4 = (bf16[128,360]{0,1:T(8,128)(2,1)S(1)}, bf16[128,360]{0,1:T(8,128)(2,1)}, u32[]{:S(2)}) copy-start(bf16[128,360]{0,1:T(8,128)(2,1)} %param.14) | copy-start | bytes 276484
  35.4 45.0 %copy-start.9 = (s32[128,4]{0,1:T(4,128)S(1)}, s32[128,4]{0,1:T(4,128)}, u32[]{:S(2)}) copy-start(s32[128,4]{0,1:T(4,128)} %param.23) | copy-start | bytes 6148
  35.4 63.6 %copy-start.7 = (f32[2880]{0:T(1024)S(1)}, f32[2880]{0:T(1024)}, u32[]{:S(2)}) copy-start(f32[2880]{0:T(1024)} %param.22) | copy-start | bytes 34564
  75.9 21.5 %all-to-all-start.1 = ((bf16[8,128,360]{1,2,0:T(8,128)(2,1)}), bf16[8,128,360]{1,2,0:T(8,128)(2,1)}, u32[]{:S(2)}, u32[]{:S(2)}) async-start(bf16[8,128,360]{1,2,0:T(8,128)(2,1)} %broadcast_in_dim.49), calls=%async_computation.1 | async-start | bytes 1474560 | tf_op jit(solution)/shard_map/all_to_all | solution.py:115
  119.2 51.5 %all-to-all-start.2 = ((bf16[32,16,2880]{2,1,0:T(8,128)(2,1)}), bf16[32,16,2880]{2,1,0:T(8,128)(2,1)}, u32[]{:S(2)}, u32[]{:S(2)}) async-start(bf16[32,16,2880]{2,1,0:T(8,128)(2,1)} %get-tuple-element.8), calls=%async_computation.2 | async-start | bytes 6029312 | tf_op jit(solution)/shard_map/all_to_all | solution.py:145
  132.1 117.5 %reduce-scatter.6.cloned.1.call-start = ((), (), s32[]{:S(2)}) async-start(), calls=%async_computation.9 | async-start | bytes 3538944 | tf_op jit(solution)/shard_map/reduce_scatter | solution.py:154
  188.3 97.7 %reduce-scatter.8.cloned.1.call-start = ((), (), s32[]{:S(2)}) async-start(), calls=%async_computation.10 | async-start | bytes 3538944 | tf_op jit(solution)/shard_map/reduce_scatter | solution.py:154
  188.4 46.1 %copy-start.12 = (bf16[1,2880,360]{1,2,0:T(8,128)(2,1)S(1)}, bf16[1,2880,360]{1,2,0:T(8,128)(2,1)}, u32[]{:S(2)}) copy-start(bf16[1,2880,360]{1,2,0:T(8,128)(2,1)} %param.25) | copy-start | bytes 6220804
  232.8 1.7 copy-start.1
  249.6 47.2 %copy-start.10 = (f32[128,4]{0,1:T(4,128)S(1)}, f32[128,4]{0,1:T(4,128)}, u32[]{:S(2)}) copy-start(f32[128,4]{0,1:T(4,128)} %param.24) | copy-start | bytes 6148
  249.7 36.4 %all-to-all-start.3 = ((bf16[32,16,360]{2,1,0:T(8,128)(2,1)}), bf16[32,16,360]{2,1,0:T(8,128)(2,1)S(1)}, u32[]{:S(2)}, u32[]{:S(2)}) async-start(bf16[32,16,360]{2,1,0:T(8,128)(2,1)} %bitcast.247), calls=%async_computation.4 | async-start | bytes 786432 | tf_op jit(solution)/shard_map/all_to_all | solution.py:155
  286.0 21.0 %all-to-all-start.5 = ((bf16[32,16,360]{2,1,0:T(8,128)(2,1)}), bf16[32,16,360]{2,1,0:T(8,128)(2,1)}, u32[]{:S(2)}, u32[]{:S(2)}) async-start(bf16[32,16,360]{2,1,0:T(8,128)(2,1)} %bitcast.248), calls=%async_computation.7 | async-start | bytes 786432 | tf_op jit(solution)/shard_map/all_to_all | solution.py:155
Sparse Core Ops, SparseCore 0:
  37.8 36.0 reduce-scatter.9
  188.4 37.1 reduce-scatter.5
  249.8 36.2 reduce-scatter.7

commit v5 on v3

--- a/solution.py
+++ b/solution.py
@@ -1,6 +1,7 @@
 import jax
 import jax.numpy as jnp
 from jax import lax
+from jax.experimental.layout import Layout, with_layout_constraint
 from jax.sharding import PartitionSpec as P
 
 D = 2880
@@ -120,27 +121,29 @@
     local_e = w_gate.shape[0]
     experts_all = local_e * seq_count
     cap = 2 * rows * topk // experts_all
+    chunks = 2
+    part = cap // chunks
     flat_routes = routes.reshape(-1)
     onehot = (flat_routes[:, None] == jnp.arange(experts_all, dtype=jnp.int32)[None, :]).astype(
         jnp.int32
     )
     rank = jnp.sum(onehot * (jnp.cumsum(onehot, 0) - 1), 1)
-    slot = flat_routes * cap + rank
+    slot = (rank // part) * (experts_all * part) + flat_routes * part + rank % part
     source = (
         jnp.full((experts_all * cap,), rows, jnp.int32)
         .at[slot]
         .set(jnp.arange(rows * topk, dtype=jnp.int32) // topk)
-    )
-    picks = (source[:, None] == jnp.arange(rows, dtype=jnp.int32)[None, :]).astype(jnp.bfloat16)
-    outgoing_rows = jnp.dot(picks, normed_full, preferred_element_type=jnp.float32).astype(
-        jnp.bfloat16
-    ).reshape(seq_count, local_e, cap, D)
+    ).reshape(chunks, experts_all * part)
+    token_ids = jnp.arange(rows, dtype=jnp.int32)
     w_down_split = w_down.reshape(local_e, w_down.shape[1], tp_count, cols)
-    chunks = 2
-    part = cap // chunks
+    row_major2 = Layout(major_to_minor=(0, 1))
     pieces = []
     for c in range(chunks):
-        sent = outgoing_rows[:, :, c * part:(c + 1) * part].reshape(seq_count, local_e * part, D)
+        picks = (source[c][:, None] == token_ids[None, :]).astype(jnp.bfloat16)
+        sent = jnp.dot(picks, normed_full, preferred_element_type=jnp.float32).astype(
+            jnp.bfloat16
+        )
+        sent = with_layout_constraint(sent, row_major2).reshape(seq_count, local_e * part, D)
         arrived = lax.all_to_all(sent, "seq", split_axis=0, concat_axis=0, tiled=True)
         arrived = arrived.reshape(seq_count, local_e, part, D)
         hidden = jnp.einsum("sexd,edf->sexf", arrived, w_gate, preferred_element_type=jnp.float32)
@@ -149,6 +152,7 @@
         down = jnp.einsum(
             "sexf,efjk->jsexk", act, w_down_split, preferred_element_type=jnp.float32
         ).astype(jnp.bfloat16)
+        down = with_layout_constraint(down, Layout(major_to_minor=(0, 1, 2, 3, 4)))
         down = down.reshape(tp_count * seq_count * local_e * part, cols)
         expert_out = lax.psum_scatter(down, "tp", scatter_dimension=0, tiled=True)
         back = lax.all_to_all(
@@ -158,8 +162,8 @@
             concat_axis=0,
             tiled=True,
         )
-        pieces.append(back.reshape(seq_count, local_e, part, cols))
-    returned = jnp.concatenate(pieces, 2)
+        pieces.append(back)
+    returned = jnp.stack(pieces, 0)
     taken = (
         returned.reshape(experts_all * cap, cols)[slot]
         .reshape(rows, topk, cols)

time: 313 us -> 291 us (0.930)
  local copies, waits for them, and re-layouts: 46.4 us -> 25.2 us
    convert_element_type x3 -> x0, local copies, waits for them, and re-layouts: 16.3 us -> none  [the longest x1 8.5 us: per_device(): jnp.dot(picks, normed_full, preferred_element_type=jnp.float32)]
    reshape x1 -> x0, local copies, waits for them, and re-layouts: 5.75 us -> none  [per_device(): outgoing_rows[:, :, c * part:(c + 1) * part]]
where the time goes in v5:
time: 291 us; the launch traced here: 289 us
  waiting for transfers between devices  91.4 us (31%)
  blocking collectives  73.7 us (25%)
  matrix products  36.2 us (12%)
  starting transfers between devices  34.3 us (12%)
  local copies, waits for them, and re-layouts  25.2 us (9%)
  between operations  14.4 us (5%)
  other arithmetic  14.1 us (5%)
    all_to_all x1, blocking collectives, per_device(): lax.all_to_all(sent, 'seq', split_axis=0, concat_axis=0, tiled=True)  43.4 us
    all_to_all x1, waiting for transfers between devices, per_device(): lax.all_to_all(sent, 'seq', split_axis=0, concat_axis=0, tiled=True)  32.7 us
    reduce_scatter x2, waiting for transfers between devices, per_device(): expert_out = lax.psum_scatter(down, 'tp', scatter_dimension=0, tiled=True)  32.4 us
    all_to_all x1, blocking collectives, per_device(): lax.all_to_all(blocks, 'tp', split_axis=0, concat_axis=0, tiled=True)  30.3 us
    all_to_all x1, waiting for transfers between devices, per_device(): lax.all_to_all(spread, 'tp', split_axis=0, concat_axis=0, tiled=True)  17.9 us
    dot_general x2, matrix products, per_device(): jnp.einsum('sexf,efjk->jsexk', act, w_down_split, preferred_element_type=...  17.2 us
    all_to_all x2, starting transfers between devices, per_device(): lax.all_to_all(expert_out.reshape(seq_count, local_e * part, cols), 'seq'...  14.9 us
    all_to_all x1, starting transfers between devices, per_device(): lax.all_to_all(outgoing, 'seq', split_axis=0, concat_axis=0, tiled=True)  8.58 us
  transfers between devices with their start and end apart: 7, of which 4 were waited for; matrix products, arithmetic and copies ran while one was open for 12% of the time, Pallas kernels for 0%

profile of v5, /device:TPU:1, one launch (start us, length us, event | category | flops | bytes accessed | tf_op | source)
XLA Modules:
  0.0 289.3 jit_solution(6840002456934189412)
XLA Ops:
  8.2 2.2 gather_fusion
  10.4 8.6 %all-to-all-start = ((bf16[32,32,1,128]{3,1,2,0:T(8,128)(2,1)}), bf16[32,32,1,128]{3,1,2,0:T(8,128)(2,1)S(1)}, u32[]{:S(2)}, u32[]{:S(2)}) async-start(bf16[32,32,1,128]{3,1,2,0:T(8,128)(2,1)} %bitcast.5), calls=%async_computation | async-start | bytes 524288 | tf_op jit(solution)/shard_map/all_to_all | solution.py:68
  19.0 1.2 dynamic_slice.7
  22.1 1.3 add_compare_fusion
  25.3 1.3 lt.56
  26.6 2.5 fusion.127
  29.2 1.6 bitcast_reduce_fusion
  34.5 30.3 %all_to_all.35 = bf16[8,128,360]{1,2,0:T(8,128)(2,1)S(1)} all-to-all(bf16[8,128,360]{1,2,0:T(8,128)(2,1)S(1)} %bitcast.227), channel_id=1, replica_groups=mesh['seq'=32,'tp'=8] {'tp'}, dimensions={0} | all-to-all | bytes 1474560 | tf_op jit(solution)/shard_map/all_to_all | solution.py:110
  65.9 4.2 %all-to-all-start.2 = ((bf16[8,128,360]{1,2,0:T(8,128)(2,1)}), bf16[8,128,360]{1,2,0:T(8,128)(2,1)}, u32[]{:S(2)}, u32[]{:S(2)}) async-start(bf16[8,128,360]{1,2,0:T(8,128)(2,1)} %broadcast_in_dim.49), calls=%async_computation.2 | async-start | bytes 1474560 | tf_op jit(solution)/shard_map/all_to_all | solution.py:115
  72.3 2.4 scatter_custom_fusion
  74.7 17.9 %all-to-all-done.2 = bf16[8,128,360]{1,2,0:T(8,128)(2,1)} async-done(((bf16[8,128,360]{1,2,0:T(8,128)(2,1)}), bf16[8,128,360]{1,2,0:T(8,128)(2,1)}, u32[]{:S(2)}, u32[]{:S(2)}) %all-to-all-start.2) | async-done | bytes 737312 | tf_op jit(solution)/shard_map/all_to_all | solution.py:115
  92.6 1.5 multiply_reduce_fusion
  94.1 1.6 fusion.18
  96.6 2.6 convolution_convert_fusion.1
  99.2 6.4 %all-to-all-start.3 = ((bf16[32,16,2880]{2,1,0:T(8,128)(2,1)}), bf16[32,16,2880]{2,1,0:T(8,128)(2,1)}, u32[]{:S(2)}, u32[]{:S(2)}) async-start(bf16[32,16,2880]{2,1,0:T(8,128)(2,1)} %bitcast.225), calls=%async_computation.3 | async-start | bytes 6029312 | tf_op jit(solution)/shard_map/all_to_all | solution.py:147
  105.8 5.6 %reshape.523 = bf16[360,8,360]{2,1,0:T(8,128)(2,1)} reshape(bf16[1,360,2880]{2,1,0:T(8,128)(2,1)} %param.27) | data formatting | bytes 4147200 | tf_op jit(solution)/shard_map/reshape.52
  111.3 32.7 %all-to-all-done.3 = bf16[32,16,2880]{2,1,0:T(8,128)(2,1)} async-done(((bf16[32,16,2880]{2,1,0:T(8,128)(2,1)}), bf16[32,16,2880]{2,1,0:T(8,128)(2,1)}, u32[]{:S(2)}, u32[]{:S(2)}) %all-to-all-start.3) | async-done | bytes 2949152 | tf_op jit(solution)/shard_map/all_to_all | solution.py:147
  144.1 5.2 %fusion.19 = f32[32,1,16,360]{3,2,0,1:T(8,128)} fusion(bf16[32,16,2880]{2,1,0:T(8,128)(2,1)} %all-to-all-done.3, bf16[1,2880,360]{1,2,0:T(8,128)(2,1)} %param.25), kind=kOutput, calls=%fused_computation.32 | convolution fusion | flops 1061683200 | bytes 5760000 | tf_op jit(solution)/shard_map/sexd,edf->sexf/dot_general | solution.py:149
  149.2 8.6 %convolution_convert_fusion.4 = bf16[32,16,8,360]{3,1,0,2:T(8,128)(2,1)} fusion(bf16[360,8,360,1]{2,1,0,3:T(8,128)(2,1)} %bitcast.230, bf16[32,16,2880]{2,1,0:T(8,128)(2,1)} %all-to-all-done.3, bf16[1,2880,360]{1,2,0:T(8,128)(2,1)} %param.26, f32[32,1,16,360]{3,2,0,1:T(8,128)} %fusion.19), kind=kOutput, calls=%fused_computation.13 | convolution fusion | flops 2126315520 | bytes 10782720 | tf_op jit(solution)/shard_map/sexf,efjk->jsexk/dot_general | solution.py:152
  157.9 2.1 convolution_convert_fusion
  160.0 43.4 %all_to_all.36 = bf16[32,16,2880]{2,1,0:T(8,128)(2,1)S(1)} all-to-all(bf16[32,16,2880]{2,1,0:T(8,128)(2,1)S(1)} %bitcast.226), channel_id=1, replica_groups=mesh['seq'=32,'tp'=8] {'seq'}, dimensions={0} | all-to-all | bytes 5898240 | tf_op jit(solution)/shard_map/all_to_all | solution.py:147
  203.4 1.7 copy-done.2
  205.0 2.6 fusion.22
  207.7 8.6 %convolution_convert_fusion.3 = bf16[32,16,8,360]{3,1,0,2:T(8,128)(2,1)} fusion(bf16[360,8,360,1]{2,1,0,3:T(8,128)(2,1)} %bitcast.231, bf16[32,16,2880]{2,1,0:T(8,128)(2,1)} %copy-done.2, bf16[1,2880,360]{1,2,0:T(8,128)(2,1)} %param.26, f32[32,1,16,360]{3,2,0,1:T(8,128)} %fusion.22), kind=kOutput, calls=%fused_computation.12 | convolution fusion | flops 2126315520 | bytes 10782720 | tf_op jit(solution)/shard_map/sexf,efjk->jsexk/dot_general | solution.py:152
  216.4 4.0 %all-to-all-start.4 = ((bf16[32,16,360]{2,1,0:T(8,128)(2,1)}), bf16[32,16,360]{2,1,0:T(8,128)(2,1)S(1)}, u32[]{:S(2)}, u32[]{:S(2)}) async-start(bf16[32,16,360]{2,1,0:T(8,128)(2,1)} %bitcast.237), calls=%async_computation.5 | async-start | bytes 786432 | tf_op jit(solution)/shard_map/all_to_all | solution.py:158
  220.4 32.4 %reduce-scatter.5.cloned.1.call-done = bf16[512,360]{1,0:T(8,128)(2,1)} async-done(((bf16[4096,360]{1,0:T(8,128)(2,1)}), bf16[512,360]{1,0:T(8,128)(2,1)}) %reduce-scatter.5.cloned.1.call-update) | async-done | bytes 368656 | tf_op jit(solution)/shard_map/reduce_scatter | solution.py:157
  252.7 10.9 %all-to-all-start.6 = ((bf16[32,16,360]{2,1,0:T(8,128)(2,1)}), bf16[32,16,360]{2,1,0:T(8,128)(2,1)}, u32[]{:S(2)}, u32[]{:S(2)}) async-start(bf16[32,16,360]{2,1,0:T(8,128)(2,1)} %bitcast.238), calls=%async_computation.8 | async-start | bytes 786432 | tf_op jit(solution)/shard_map/all_to_all | solution.py:158
  263.7 1.7 copy.84
  265.4 8.4 %all-to-all-done.6 = bf16[32,16,360]{2,1,0:T(8,128)(2,1)} async-done(((bf16[32,16,360]{2,1,0:T(8,128)(2,1)}), bf16[32,16,360]{2,1,0:T(8,128)(2,1)}, u32[]{:S(2)}, u32[]{:S(2)}) %all-to-all-start.6) | async-done | bytes 368672 | tf_op jit(solution)/shard_map/all_to_all | solution.py:158
  273.8 2.0 pad_maximum_fusion
  275.8 3.0 %gather_fusion.1 = bf16[512,360]{1,0:T(8,128)(2,1)S(1)} fusion(bf16[1024,360]{1,0:T(8,128)(2,1)} %bitcast.224, s32[1024]{0:T(1024)S(1)} %pad_clamp_fusion), kind=kCustom, calls=%fused_computation.1 | custom fusion | bytes 739328 | tf_op jit(solution)/shard_map/gather | solution.py:168
  280.0 1.7 multiply_reduce_fusion.1
  (81 shorter events, 14.7 us)
Async XLA Ops:
  7.2 26.3 %copy-start = (bf16[512,2880]{0,1:T(8,128)(2,1)S(1)}, bf16[512,2880]{0,1:T(8,128)(2,1)}, u32[]{:S(2)}) copy-start(bf16[512,2880]{0,1:T(8,128)(2,1)} %param.21) | copy-start | bytes 8847364
  10.4 18.6 %all-to-all-start = ((bf16[32,32,1,128]{3,1,2,0:T(8,128)(2,1)}), bf16[32,32,1,128]{3,1,2,0:T(8,128)(2,1)S(1)}, u32[]{:S(2)}, u32[]{:S(2)}) async-start(bf16[32,32,1,128]{3,1,2,0:T(8,128)(2,1)} %bitcast.5), calls=%async_computation | async-start | bytes 524288 | tf_op jit(solution)/shard_map/all_to_all | solution.py:68
  29.1 1.8 copy-start.7
  29.1 1.8 copy-start.12
  29.1 1.9 copy-start.9
  29.1 1.8 copy-start.3
  31.9 1.2 copy-start.6
  33.5 1.0 copy-start.4
  33.5 31.4 %copy-start.5 = (bf16[128,360]{0,1:T(8,128)(2,1)S(1)}, bf16[128,360]{0,1:T(8,128)(2,1)}, u32[]{:S(2)}) copy-start(bf16[128,360]{0,1:T(8,128)(2,1)} %param.14) | copy-start | bytes 276484
  34.4 35.7 %copy-start.10 = (s32[128,4]{0,1:T(4,128)S(1)}, s32[128,4]{0,1:T(4,128)}, u32[]{:S(2)}) copy-start(s32[128,4]{0,1:T(4,128)} %param.23) | copy-start | bytes 6148
  34.5 59.7 %copy-start.8 = (f32[2880]{0:T(1024)S(1)}, f32[2880]{0:T(1024)}, u32[]{:S(2)}) copy-start(f32[2880]{0:T(1024)} %param.22) | copy-start | bytes 34564
  65.9 26.7 %all-to-all-start.2 = ((bf16[8,128,360]{1,2,0:T(8,128)(2,1)}), bf16[8,128,360]{1,2,0:T(8,128)(2,1)}, u32[]{:S(2)}, u32[]{:S(2)}) async-start(bf16[8,128,360]{1,2,0:T(8,128)(2,1)} %broadcast_in_dim.49), calls=%async_computation.2 | async-start | bytes 1474560 | tf_op jit(solution)/shard_map/all_to_all | solution.py:115
  95.7 0.9 copy-start.1
  99.2 44.9 %all-to-all-start.3 = ((bf16[32,16,2880]{2,1,0:T(8,128)(2,1)}), bf16[32,16,2880]{2,1,0:T(8,128)(2,1)}, u32[]{:S(2)}, u32[]{:S(2)}) async-start(bf16[32,16,2880]{2,1,0:T(8,128)(2,1)} %bitcast.225), calls=%async_computation.3 | async-start | bytes 6029312 | tf_op jit(solution)/shard_map/all_to_all | solution.py:147
  105.6 110.8 %reduce-scatter.3.cloned.1.call-start = ((), (), s32[]{:S(2)}) async-start(), calls=%async_computation.9 | async-start | bytes 3538944 | tf_op jit(solution)/shard_map/reduce_scatter | solution.py:157
  157.8 94.9 %reduce-scatter.5.cloned.1.call-start = ((), (), s32[]{:S(2)}) async-start(), calls=%async_computation.10 | async-start | bytes 3538944 | tf_op jit(solution)/shard_map/reduce_scatter | solution.py:157
  160.0 45.0 %copy-start.13 = (bf16[1,2880,360]{1,2,0:T(8,128)(2,1)S(1)}, bf16[1,2880,360]{1,2,0:T(8,128)(2,1)}, u32[]{:S(2)}) copy-start(bf16[1,2880,360]{1,2,0:T(8,128)(2,1)} %param.25) | copy-start | bytes 6220804
  203.4 1.7 copy-start.2
  216.3 47.3 %copy-start.11 = (f32[128,4]{0,1:T(4,128)S(1)}, f32[128,4]{0,1:T(4,128)}, u32[]{:S(2)}) copy-start(f32[128,4]{0,1:T(4,128)} %param.24) | copy-start | bytes 6148
  216.4 36.4 %all-to-all-start.4 = ((bf16[32,16,360]{2,1,0:T(8,128)(2,1)}), bf16[32,16,360]{2,1,0:T(8,128)(2,1)S(1)}, u32[]{:S(2)}, u32[]{:S(2)}) async-start(bf16[32,16,360]{2,1,0:T(8,128)(2,1)} %bitcast.237), calls=%async_computation.5 | async-start | bytes 786432 | tf_op jit(solution)/shard_map/all_to_all | solution.py:158
  252.7 21.1 %all-to-all-start.6 = ((bf16[32,16,360]{2,1,0:T(8,128)(2,1)}), bf16[32,16,360]{2,1,0:T(8,128)(2,1)}, u32[]{:S(2)}, u32[]{:S(2)}) async-start(bf16[32,16,360]{2,1,0:T(8,128)(2,1)} %bitcast.238), calls=%async_computation.8 | async-start | bytes 786432 | tf_op jit(solution)/shard_map/all_to_all | solution.py:158
Sparse Core Ops, SparseCore 0:
  158.0 37.1 reduce-scatter.2
  216.5 36.2 reduce-scatter.4

commit v6 on v5

--- a/solution.py
+++ b/solution.py
@@ -137,17 +137,40 @@
     token_ids = jnp.arange(rows, dtype=jnp.int32)
     w_down_split = w_down.reshape(local_e, w_down.shape[1], tp_count, cols)
     row_major2 = Layout(major_to_minor=(0, 1))
+    tp_here = lax.axis_index("tp")
+    gain_here = lax.dynamic_slice_in_dim(norm_gain, tp_here * cols, cols)
+    normed_own = (resid_wide * scale_rows[:, None] * gain_here[None, :]).astype(jnp.bfloat16)
+    w_gate_in = w_gate[0].reshape(tp_count, cols, w_gate.shape[2])
+    w_up_in = w_up[0].reshape(tp_count, cols, w_up.shape[2])
     pieces = []
     for c in range(chunks):
         picks = (source[c][:, None] == token_ids[None, :]).astype(jnp.bfloat16)
-        sent = jnp.dot(picks, normed_full, preferred_element_type=jnp.float32).astype(
-            jnp.bfloat16
-        )
-        sent = with_layout_constraint(sent, row_major2).reshape(seq_count, local_e * part, D)
-        arrived = lax.all_to_all(sent, "seq", split_axis=0, concat_axis=0, tiled=True)
-        arrived = arrived.reshape(seq_count, local_e, part, D)
-        hidden = jnp.einsum("sexd,edf->sexf", arrived, w_gate, preferred_element_type=jnp.float32)
-        lin = jnp.einsum("sexd,edf->sexf", arrived, w_up, preferred_element_type=jnp.float32)
+        if c == 0:
+            sent = jnp.dot(picks, normed_full, preferred_element_type=jnp.float32).astype(
+                jnp.bfloat16
+            )
+            sent = with_layout_constraint(sent, row_major2).reshape(seq_count, local_e * part, D)
+            arrived = lax.all_to_all(sent, "seq", split_axis=0, concat_axis=0, tiled=True)
+            arrived = arrived.reshape(seq_count, local_e, part, D)
+            hidden = jnp.einsum(
+                "sexd,edf->sexf", arrived, w_gate, preferred_element_type=jnp.float32
+            )
+            lin = jnp.einsum("sexd,edf->sexf", arrived, w_up, preferred_element_type=jnp.float32)
+        else:
+            sent = jnp.dot(picks, normed_own, preferred_element_type=jnp.float32).astype(
+                jnp.bfloat16
+            )
+            sent = with_layout_constraint(sent, row_major2).reshape(seq_count, local_e * part, cols)
+            arrived = lax.all_to_all(sent, "seq", split_axis=0, concat_axis=0, tiled=True)
+            blocks_in = lax.all_gather(
+                arrived.reshape(seq_count * local_e * part, cols), "tp", axis=0, tiled=False
+            )
+            hidden = jnp.einsum(
+                "jmk,jkf->mf", blocks_in, w_gate_in, preferred_element_type=jnp.float32
+            ).reshape(seq_count, local_e, part, -1)
+            lin = jnp.einsum(
+                "jmk,jkf->mf", blocks_in, w_up_in, preferred_element_type=jnp.float32
+            ).reshape(seq_count, local_e, part, -1)
         act = (hidden * jax.nn.sigmoid(1.702 * hidden) * (lin + 1.0)).astype(jnp.bfloat16)
         down = jnp.einsum(
             "sexf,efjk->jsexk", act, w_down_split, preferred_element_type=jnp.float32

time: 291 us -> 297 us (1.021)
  local copies, waits for them, and re-layouts: 25.2 us -> 36.9 us
  blocking collectives: 73.7 us -> 67.2 us
  waiting for transfers between devices: 91.4 us -> 97.6 us
  starting transfers between devices: 34.3 us -> 28.4 us
    all_to_all x1, blocking collectives: 43.4 us -> 16.3 us  [per_device(): lax.all_to_all(sent, 'seq', split_axis=0, concat_axis=0, tiled=True)]
    all_to_all x0 -> x1, blocking collectives: none -> 20.6 us  [per_device(): lax.all_to_all(expert_out.reshape(seq_count, local_e * part, cols), 'seq'...]
    another operation x2 -> x5, local copies, waits for them, and re-layouts: 5.57 us -> 14.7 us
    reduce_scatter x2, waiting for transfers between devices: 32.4 us -> 38.9 us  [per_device(): expert_out = lax.psum_scatter(down, 'tp', scatter_dimension=0, tiled=True)]
    dot_general x0 -> x2, matrix products: none -> 5.78 us  [the longest x1 5.43 us: per_device(): jnp.einsum('jmk,jkf->mf', blocks_in, w_gate_in, preferred_element_type=jn...]
    all_gather x0 -> x1, local copies, waits for them, and re-layouts: none -> 5.04 us  [per_device(): lax.all_gather(arrived.reshape(seq_count * local_e * part, cols), 'tp', a...]
    all_to_all x2 -> x1, starting transfers between devices: 14.9 us -> 10.6 us  [per_device(): lax.all_to_all(expert_out.reshape(seq_count, local_e * part, cols), 'seq'...]
    dot_general x2 -> x1, matrix products: 7.8 us -> 5.16 us  [per_device(): jnp.einsum('sexd,edf->sexf', arrived, w_gate, preferred_element_type=jnp....]
  transfers between devices with their start and end apart: 7 -> 7, of which waited for: 4 -> 5; matrix products, arithmetic and copies ran while one was open for 12% -> 23% of each run, Pallas kernels for 0% -> 0%
where the time goes in v6:
time: 297 us; the launch traced here: 296 us
  waiting for transfers between devices  97.6 us (33%)
  blocking collectives  67.2 us (23%)
  matrix products  37.4 us (13%)
  local copies, waits for them, and re-layouts  36.9 us (12%)
  starting transfers between devices  28.4 us (10%)
  other arithmetic  14.1 us (5%)
  between operations  14.1 us (5%)
    reduce_scatter x2, waiting for transfers between devices, per_device(): expert_out = lax.psum_scatter(down, 'tp', scatter_dimension=0, tiled=True)  38.9 us
    all_to_all x1, waiting for transfers between devices, per_device(): lax.all_to_all(sent, 'seq', split_axis=0, concat_axis=0, tiled=True)  32.4 us
    all_to_all x1, blocking collectives, per_device(): lax.all_to_all(blocks, 'tp', split_axis=0, concat_axis=0, tiled=True)  30.3 us
    all_to_all x1, blocking collectives, per_device(): lax.all_to_all(expert_out.reshape(seq_count, local_e * part, cols), 'seq'...  20.6 us
    all_to_all x1, waiting for transfers between devices, per_device(): lax.all_to_all(spread, 'tp', split_axis=0, concat_axis=0, tiled=True)  17.7 us
    dot_general x2, matrix products, per_device(): jnp.einsum('sexf,efjk->jsexk', act, w_down_split, preferred_element_type=...  17.4 us
    all_to_all x1, blocking collectives, per_device(): lax.all_to_all(sent, 'seq', split_axis=0, concat_axis=0, tiled=True)  16.3 us
    all_to_all x1, starting transfers between devices, per_device(): lax.all_to_all(expert_out.reshape(seq_count, local_e * part, cols), 'seq'...  10.6 us
  transfers between devices with their start and end apart: 7, of which 5 were waited for; matrix products, arithmetic and copies ran while one was open for 23% of the time, Pallas kernels for 0%

profile of v6, /device:TPU:1, one launch (start us, length us, event | category | flops | bytes accessed | tf_op | source)
XLA Modules:
  0.0 295.7 jit_solution(8392931168094025753)
XLA Ops:
  8.2 2.2 gather_fusion
  10.4 8.6 %all-to-all-start = ((bf16[32,32,1,128]{3,1,2,0:T(8,128)(2,1)}), bf16[32,32,1,128]{3,1,2,0:T(8,128)(2,1)S(1)}, u32[]{:S(2)}, u32[]{:S(2)}) async-start(bf16[32,32,1,128]{3,1,2,0:T(8,128)(2,1)} %bitcast.5), calls=%async_computation | async-start | bytes 524288 | tf_op jit(solution)/shard_map/all_to_all | solution.py:68
  25.3 1.3 lt.59
  26.6 2.5 fusion.132
  29.2 1.6 bitcast_reduce_fusion
  34.5 30.3 %all_to_all.35 = bf16[8,128,360]{1,2,0:T(8,128)(2,1)S(1)} all-to-all(bf16[8,128,360]{1,2,0:T(8,128)(2,1)S(1)} %bitcast.212), channel_id=1, replica_groups=mesh['seq'=32,'tp'=8] {'tp'}, dimensions={0} | all-to-all | bytes 1474560 | tf_op jit(solution)/shard_map/all_to_all | solution.py:110
  65.9 4.2 %all-to-all-start.2 = ((bf16[8,128,360]{1,2,0:T(8,128)(2,1)}), bf16[8,128,360]{1,2,0:T(8,128)(2,1)}, u32[]{:S(2)}, u32[]{:S(2)}) async-start(bf16[8,128,360]{1,2,0:T(8,128)(2,1)} %broadcast_in_dim.49), calls=%async_computation.2 | async-start | bytes 1474560 | tf_op jit(solution)/shard_map/all_to_all | solution.py:115
  72.4 2.4 scatter_custom_fusion
  74.9 17.7 %all-to-all-done.2 = bf16[8,128,360]{1,2,0:T(8,128)(2,1)} async-done(((bf16[8,128,360]{1,2,0:T(8,128)(2,1)}), bf16[8,128,360]{1,2,0:T(8,128)(2,1)}, u32[]{:S(2)}, u32[]{:S(2)}) %all-to-all-start.2) | async-done | bytes 737312 | tf_op jit(solution)/shard_map/all_to_all | solution.py:115
  92.6 1.5 multiply_reduce_fusion
  94.5 16.3 %all_to_all.36 = bf16[32,16,360]{2,1,0:T(8,128)(2,1)S(1)} all-to-all(bf16[32,16,360]{2,1,0:T(8,128)(2,1)S(1)} %bitcast.221), channel_id=1, replica_groups=mesh['seq'=32,'tp'=8] {'seq'}, dimensions={0} | all-to-all | bytes 737280 | tf_op jit(solution)/shard_map/all_to_all | solution.py:164
  111.7 1.6 fusion.18
  113.3 2.6 convolution_convert_fusion
  115.9 4.7 %all-to-all-start.3 = ((bf16[32,16,2880]{2,1,0:T(8,128)(2,1)}), bf16[32,16,2880]{2,1,0:T(8,128)(2,1)}, u32[]{:S(2)}, u32[]{:S(2)}) async-start(bf16[32,16,2880]{2,1,0:T(8,128)(2,1)} %bitcast.211), calls=%async_computation.3 | async-start | bytes 6029312 | tf_op jit(solution)/shard_map/all_to_all | solution.py:153
  120.8 5.5 %reshape.528 = bf16[360,8,360]{2,1,0:T(8,128)(2,1)} reshape(bf16[1,360,2880]{2,1,0:T(8,128)(2,1)} %param.27) | data formatting | bytes 4147200 | tf_op jit(solution)/shard_map/reshape.53
  126.4 32.4 %all-to-all-done.3 = bf16[32,16,2880]{2,1,0:T(8,128)(2,1)} async-done(((bf16[32,16,2880]{2,1,0:T(8,128)(2,1)}), bf16[32,16,2880]{2,1,0:T(8,128)(2,1)}, u32[]{:S(2)}, u32[]{:S(2)}) %all-to-all-start.3) | async-done | bytes 2949152 | tf_op jit(solution)/shard_map/all_to_all | solution.py:153
  158.8 5.2 %fusion.19 = f32[32,1,16,360]{3,2,0,1:T(8,128)} fusion(bf16[32,16,2880]{2,1,0:T(8,128)(2,1)} %all-to-all-done.3, bf16[1,2880,360]{1,2,0:T(8,128)(2,1)} %param.25), kind=kOutput, calls=%fused_computation.31 | convolution fusion | flops 1061683200 | bytes 5760000 | tf_op jit(solution)/shard_map/sexd,edf->sexf/dot_general | solution.py:155
  164.0 8.6 %convolution_convert_fusion.3 = bf16[32,16,8,360]{3,1,0,2:T(8,128)(2,1)} fusion(bf16[360,8,360,1]{2,1,0,3:T(8,128)(2,1)} %bitcast.217, bf16[32,16,2880]{2,1,0:T(8,128)(2,1)} %all-to-all-done.3, bf16[1,2880,360]{1,2,0:T(8,128)(2,1)} %param.26, f32[32,1,16,360]{3,2,0,1:T(8,128)} %fusion.19), kind=kOutput, calls=%fused_computation.16 | convolution fusion | flops 2126315520 | bytes 10782720 | tf_op jit(solution)/shard_map/sexf,efjk->jsexk/dot_general | solution.py:175
  172.6 4.1 %copy.136 = bf16[1,2880,360]{2,1,0:T(8,128)(2,1)} copy(bf16[1,2880,360]{1,2,0:T(8,128)(2,1)} %param.25) | data formatting | bytes 4147200 | tf_op jit(solution)/shard_map/reshape;squeeze | solution.py:143
  176.8 4.1 %copy.137 = bf16[1,2880,360]{2,1,0:T(8,128)(2,1)} copy(bf16[1,2880,360]{1,2,0:T(8,128)(2,1)} %param.26) | data formatting | bytes 4147200 | tf_op jit(solution)/shard_map/reshape;squeeze | solution.py:144
  180.9 5.0 %copy.113 = bf16[8,512,360]{2,0,1:T(8,128)(2,1)} copy(bf16[8,512,360]{1,2,0:T(8,128)(2,1)} %all-gather.2.cloned.1.call-done) | data formatting | bytes 5898240 | tf_op jit(solution)/shard_map/all_gather | solution.py:165
  185.9 5.4 %fusion.22 = f32[32,16,360]{2,1,0:T(8,128)} fusion(bf16[8,360,360,1]{2,1,0,3:T(8,128)(2,1)} %bitcast.220, bf16[32,16,8,360]{3,2,1,0:T(8,128)(2,1)} %bitcast.215), kind=kOutput, calls=%fused_computation.32 | convolution fusion | flops 1061683200 | bytes 5760000 | tf_op jit(solution)/shard_map/jmk,jkf->mf/dot_general | solution.py:168
  191.3 8.8 %convolution_convert_fusion.2 = bf16[32,16,8,360]{3,1,0,2:T(8,128)(2,1)} fusion(bf16[360,8,360,1]{2,1,0,3:T(8,128)(2,1)} %bitcast.218, bf16[8,360,360,1]{2,1,0,3:T(8,128)(2,1)} %bitcast.219, bf16[32,16,8,360]{3,2,1,0:T(8,128)(2,1)} %bitcast.216, f32[32,16,360]{2,1,0:T(8,128)} %fusion.22), kind=kOutput, calls=%fused_computation.15 | convolution fusion | flops 2126315520 | bytes 10782720 | tf_op jit(solution)/shard_map/sexf,efjk->jsexk/dot_general | solution.py:175
  200.2 10.4 %reduce-scatter.3.cloned.1.call-done = bf16[512,360]{1,0:T(8,128)(2,1)} async-done(((bf16[4096,360]{1,0:T(8,128)(2,1)}), bf16[512,360]{1,0:T(8,128)(2,1)}) %reduce-scatter.3.cloned.1.call-update) | async-done | bytes 368656 | tf_op jit(solution)/shard_map/reduce_scatter | solution.py:180
  210.5 20.6 %all_to_all.37 = bf16[32,16,360]{2,1,0:T(8,128)(2,1)S(1)} all-to-all(bf16[32,16,360]{2,1,0:T(8,128)(2,1)} %bitcast.228), channel_id=1, replica_groups=mesh['seq'=32,'tp'=8] {'seq'}, dimensions={0} | all-to-all | bytes 737280 | tf_op jit(solution)/shard_map/all_to_all | solution.py:181
  231.1 28.6 %reduce-scatter.5.cloned.1.call-done = bf16[512,360]{1,0:T(8,128)(2,1)} async-done(((bf16[4096,360]{1,0:T(8,128)(2,1)}), bf16[512,360]{1,0:T(8,128)(2,1)}) %reduce-scatter.5.cloned.1.call-update) | async-done | bytes 368656 | tf_op jit(solution)/shard_map/reduce_scatter | solution.py:180
  259.7 10.6 %all-to-all-start.6 = ((bf16[32,16,360]{2,1,0:T(8,128)(2,1)}), bf16[32,16,360]{2,1,0:T(8,128)(2,1)}, u32[]{:S(2)}, u32[]{:S(2)}) async-start(bf16[32,16,360]{2,1,0:T(8,128)(2,1)} %bitcast.229), calls=%async_computation.8 | async-start | bytes 786432 | tf_op jit(solution)/shard_map/all_to_all | solution.py:181
  270.4 1.7 copy.121
  272.1 8.4 %all-to-all-done.6 = bf16[32,16,360]{2,1,0:T(8,128)(2,1)} async-done(((bf16[32,16,360]{2,1,0:T(8,128)(2,1)}), bf16[32,16,360]{2,1,0:T(8,128)(2,1)}, u32[]{:S(2)}, u32[]{:S(2)}) %all-to-all-start.6) | async-done | bytes 368672 | tf_op jit(solution)/shard_map/all_to_all | solution.py:181
  280.5 2.0 pad_maximum_fusion
  282.5 3.0 %gather_fusion.1 = bf16[512,360]{1,0:T(8,128)(2,1)S(1)} fusion(bf16[1024,360]{1,0:T(8,128)(2,1)} %bitcast.210, s32[1024]{0:T(1024)S(1)} %pad_clamp_fusion), kind=kCustom, calls=%fused_computation.1 | custom fusion | bytes 739328 | tf_op jit(solution)/shard_map/gather | solution.py:191
  286.6 1.7 multiply_reduce_fusion.1
  (82 shorter events, 17.8 us)
Async XLA Ops:
  7.2 26.3 %copy-start = (bf16[512,2880]{0,1:T(8,128)(2,1)S(1)}, bf16[512,2880]{0,1:T(8,128)(2,1)}, u32[]{:S(2)}) copy-start(bf16[512,2880]{0,1:T(8,128)(2,1)} %param.21) | copy-start | bytes 8847364
  10.4 18.6 %all-to-all-start = ((bf16[32,32,1,128]{3,1,2,0:T(8,128)(2,1)}), bf16[32,32,1,128]{3,1,2,0:T(8,128)(2,1)S(1)}, u32[]{:S(2)}, u32[]{:S(2)}) async-start(bf16[32,32,1,128]{3,1,2,0:T(8,128)(2,1)} %bitcast.5), calls=%async_computation | async-start | bytes 524288 | tf_op jit(solution)/shard_map/all_to_all | solution.py:68
  29.1 1.8 copy-start.6
  29.1 1.8 copy-start.10
  29.1 1.9 copy-start.7
  29.1 1.8 copy-start.1
  31.9 1.2 copy-start.4
  33.5 1.0 copy-start.2
  33.5 31.4 %copy-start.3 = (bf16[128,360]{0,1:T(8,128)(2,1)S(1)}, bf16[128,360]{0,1:T(8,128)(2,1)}, u32[]{:S(2)}) copy-start(bf16[128,360]{0,1:T(8,128)(2,1)} %param.14) | copy-start | bytes 276484
  34.4 35.7 %copy-start.8 = (s32[128,4]{0,1:T(4,128)S(1)}, s32[128,4]{0,1:T(4,128)}, u32[]{:S(2)}) copy-start(s32[128,4]{0,1:T(4,128)} %param.23) | copy-start | bytes 6148
  34.5 37.7 %copy-start.5 = (f32[2880]{0:T(1024)S(1)}, f32[2880]{0:T(1024)}, u32[]{:S(2)}) copy-start(f32[2880]{0:T(1024)} %param.22) | copy-start | bytes 34564
  65.9 26.7 %all-to-all-start.2 = ((bf16[8,128,360]{1,2,0:T(8,128)(2,1)}), bf16[8,128,360]{1,2,0:T(8,128)(2,1)}, u32[]{:S(2)}, u32[]{:S(2)}) async-start(bf16[8,128,360]{1,2,0:T(8,128)(2,1)} %broadcast_in_dim.49), calls=%async_computation.2 | async-start | bytes 1474560 | tf_op jit(solution)/shard_map/all_to_all | solution.py:115
  70.1 110.7 %all-gather.2.cloned.1.call-start = ((), (), s32[]{:S(2)}) async-start(), calls=%async_computation.10 | async-start | bytes 3317760 | tf_op jit(solution)/shard_map/all_gather | solution.py:165
  115.9 42.9 %all-to-all-start.3 = ((bf16[32,16,2880]{2,1,0:T(8,128)(2,1)}), bf16[32,16,2880]{2,1,0:T(8,128)(2,1)}, u32[]{:S(2)}, u32[]{:S(2)}) async-start(bf16[32,16,2880]{2,1,0:T(8,128)(2,1)} %bitcast.211), calls=%async_computation.3 | async-start | bytes 6029312 | tf_op jit(solution)/shard_map/all_to_all | solution.py:153
  120.6 90.0 %reduce-scatter.3.cloned.1.call-start = ((), (), s32[]{:S(2)}) async-start(), calls=%async_computation.9 | async-start | bytes 3538944 | tf_op jit(solution)/shard_map/reduce_scatter | solution.py:180
  172.6 87.1 %reduce-scatter.5.cloned.1.call-start = ((), (), s32[]{:S(2)}) async-start(), calls=%async_computation.11 | async-start | bytes 3538944 | tf_op jit(solution)/shard_map/reduce_scatter | solution.py:180
  200.1 70.1 %copy-start.9 = (f32[128,4]{0,1:T(4,128)S(1)}, f32[128,4]{0,1:T(4,128)}, u32[]{:S(2)}) copy-start(f32[128,4]{0,1:T(4,128)} %param.24) | copy-start | bytes 6148
  259.7 20.8 %all-to-all-start.6 = ((bf16[32,16,360]{2,1,0:T(8,128)(2,1)}), bf16[32,16,360]{2,1,0:T(8,128)(2,1)}, u32[]{:S(2)}, u32[]{:S(2)}) async-start(bf16[32,16,360]{2,1,0:T(8,128)(2,1)} %bitcast.229), calls=%async_computation.8 | async-start | bytes 786432 | tf_op jit(solution)/shard_map/all_to_all | solution.py:181
Sparse Core Ops, SparseCore 0:
  111.8 34.3 all-gather.1
  172.7 37.7 reduce-scatter.2
  213.1 46.5 reduce-scatter.4

commit v7 on v6

--- a/solution.py
+++ b/solution.py
@@ -140,8 +140,6 @@
     tp_here = lax.axis_index("tp")
     gain_here = lax.dynamic_slice_in_dim(norm_gain, tp_here * cols, cols)
     normed_own = (resid_wide * scale_rows[:, None] * gain_here[None, :]).astype(jnp.bfloat16)
-    w_gate_in = w_gate[0].reshape(tp_count, cols, w_gate.shape[2])
-    w_up_in = w_up[0].reshape(tp_count, cols, w_up.shape[2])
     pieces = []
     for c in range(chunks):
         picks = (source[c][:, None] == token_ids[None, :]).astype(jnp.bfloat16)
@@ -165,12 +163,11 @@
             blocks_in = lax.all_gather(
                 arrived.reshape(seq_count * local_e * part, cols), "tp", axis=0, tiled=False
             )
+            arrived = blocks_in.transpose(1, 0, 2).reshape(seq_count, local_e, part, D)
             hidden = jnp.einsum(
-                "jmk,jkf->mf", blocks_in, w_gate_in, preferred_element_type=jnp.float32
-            ).reshape(seq_count, local_e, part, -1)
-            lin = jnp.einsum(
-                "jmk,jkf->mf", blocks_in, w_up_in, preferred_element_type=jnp.float32
-            ).reshape(seq_count, local_e, part, -1)
+                "sexd,edf->sexf", arrived, w_gate, preferred_element_type=jnp.float32
+            )
+            lin = jnp.einsum("sexd,edf->sexf", arrived, w_up, preferred_element_type=jnp.float32)
         act = (hidden * jax.nn.sigmoid(1.702 * hidden) * (lin + 1.0)).astype(jnp.bfloat16)
         down = jnp.einsum(
             "sexf,efjk->jsexk", act, w_down_split, preferred_element_type=jnp.float32

time: 297 us -> 297 us (level)
    dot_general x1 -> x0, matrix products: 5.43 us -> none  [per_device(): jnp.einsum('jmk,jkf->mf', blocks_in, w_gate_in, preferred_element_type=jn...]
    dot_general x1 -> x2, matrix products: 5.16 us -> 10.4 us  [per_device(): jnp.einsum('sexd,edf->sexf', arrived, w_gate, preferred_element_type=jnp....]
    all_gather x1 -> x0, local copies, waits for them, and re-layouts: 5.04 us -> none  [per_device(): lax.all_gather(arrived.reshape(seq_count * local_e * part, cols), 'tp', a...]
    transpose x0 -> x1, local copies, waits for them, and re-layouts: none -> 4.99 us  [per_device(): arrived = blocks_in.transpose(1, 0, 2).reshape(seq_count, local_e, part, D)]
    another operation x4 -> x3, local copies, waits for them, and re-layouts: 13.8 us -> 12 us
  transfers between devices with their start and end apart: 7 -> 7, of which waited for: 5 -> 5; matrix products, arithmetic and copies ran while one was open for 23% -> 22% of each run, Pallas kernels for 0% -> 0%
where the time goes in v7:
time: 297 us; the launch traced here: 296 us
  waiting for transfers between devices  99.5 us (34%)
  blocking collectives  67.3 us (23%)
  matrix products  37.1 us (12%)
  local copies, waits for them, and re-layouts  35 us (12%)
  starting transfers between devices  28.5 us (10%)
  other arithmetic  14.1 us (5%)
  between operations  14.1 us (5%)
    reduce_scatter x2, waiting for transfers between devices, per_device(): expert_out = lax.psum_scatter(down, 'tp', scatter_dimension=0, tiled=True)  40.9 us
    all_to_all x1, waiting for transfers between devices, per_device(): lax.all_to_all(sent, 'seq', split_axis=0, concat_axis=0, tiled=True)  32.4 us
    all_to_all x1, blocking collectives, per_device(): lax.all_to_all(blocks, 'tp', split_axis=0, concat_axis=0, tiled=True)  30.3 us
    all_to_all x1, blocking collectives, per_device(): lax.all_to_all(expert_out.reshape(seq_count, local_e * part, cols), 'seq'...  20.7 us
    all_to_all x1, waiting for transfers between devices, per_device(): lax.all_to_all(spread, 'tp', split_axis=0, concat_axis=0, tiled=True)  17.7 us
    dot_general x2, matrix products, per_device(): jnp.einsum('sexf,efjk->jsexk', act, w_down_split, preferred_element_type=...  17.3 us
    all_to_all x1, blocking collectives, per_device(): lax.all_to_all(sent, 'seq', split_axis=0, concat_axis=0, tiled=True)  16.3 us
    another operation x3, local copies, waits for them, and re-layouts  12 us
  transfers between devices with their start and end apart: 7, of which 5 were waited for; matrix products, arithmetic and copies ran while one was open for 22% of the time, Pallas kernels for 0%

profile of v7, /device:TPU:1, one launch (start us, length us, event | category | flops | bytes accessed | tf_op | source)
XLA Modules:
  0.0 295.8 jit_solution(9373696623638786293)
XLA Ops:
  8.2 2.2 gather_fusion
  10.4 8.6 %all-to-all-start = ((bf16[32,32,1,128]{3,1,2,0:T(8,128)(2,1)}), bf16[32,32,1,128]{3,1,2,0:T(8,128)(2,1)S(1)}, u32[]{:S(2)}, u32[]{:S(2)}) async-start(bf16[32,32,1,128]{3,1,2,0:T(8,128)(2,1)} %bitcast.5), calls=%async_computation | async-start | bytes 524288 | tf_op jit(solution)/shard_map/all_to_all | solution.py:68
  22.1 1.3 add_compare_fusion
  25.3 1.3 lt.59
  26.6 2.5 fusion.133
  29.2 1.6 bitcast_reduce_fusion
  34.5 30.3 %all_to_all.35 = bf16[8,128,360]{1,2,0:T(8,128)(2,1)S(1)} all-to-all(bf16[8,128,360]{1,2,0:T(8,128)(2,1)S(1)} %bitcast.227), channel_id=1, replica_groups=mesh['seq'=32,'tp'=8] {'tp'}, dimensions={0} | all-to-all | bytes 1474560 | tf_op jit(solution)/shard_map/all_to_all | solution.py:110
  65.9 4.2 %all-to-all-start.2 = ((bf16[8,128,360]{1,2,0:T(8,128)(2,1)}), bf16[8,128,360]{1,2,0:T(8,128)(2,1)}, u32[]{:S(2)}, u32[]{:S(2)}) async-start(bf16[8,128,360]{1,2,0:T(8,128)(2,1)} %broadcast_in_dim.49), calls=%async_computation.2 | async-start | bytes 1474560 | tf_op jit(solution)/shard_map/all_to_all | solution.py:115
  72.4 2.4 scatter_custom_fusion
  74.9 17.7 %all-to-all-done.2 = bf16[8,128,360]{1,2,0:T(8,128)(2,1)} async-done(((bf16[8,128,360]{1,2,0:T(8,128)(2,1)}), bf16[8,128,360]{1,2,0:T(8,128)(2,1)}, u32[]{:S(2)}, u32[]{:S(2)}) %all-to-all-start.2) | async-done | bytes 737312 | tf_op jit(solution)/shard_map/all_to_all | solution.py:115
  92.6 1.5 multiply_reduce_fusion
  94.5 16.3 %all_to_all.36 = bf16[32,16,360]{2,1,0:T(8,128)(2,1)S(1)} all-to-all(bf16[32,16,360]{2,1,0:T(8,128)(2,1)S(1)} %bitcast.233), channel_id=1, replica_groups=mesh['seq'=32,'tp'=8] {'seq'}, dimensions={0} | all-to-all | bytes 737280 | tf_op jit(solution)/shard_map/all_to_all | solution.py:162
  111.8 1.6 fusion.18
  113.3 2.6 convolution_convert_fusion
  115.9 4.7 %all-to-all-start.3 = ((bf16[32,16,2880]{2,1,0:T(8,128)(2,1)}), bf16[32,16,2880]{2,1,0:T(8,128)(2,1)}, u32[]{:S(2)}, u32[]{:S(2)}) async-start(bf16[32,16,2880]{2,1,0:T(8,128)(2,1)} %bitcast.226), calls=%async_computation.3 | async-start | bytes 6029312 | tf_op jit(solution)/shard_map/all_to_all | solution.py:151
  120.8 5.6 %reshape.526 = bf16[360,8,360]{2,1,0:T(8,128)(2,1)} reshape(bf16[1,360,2880]{2,1,0:T(8,128)(2,1)} %param.27) | data formatting | bytes 4147200 | tf_op jit(solution)/shard_map/reshape.52
  126.4 32.4 %all-to-all-done.3 = bf16[32,16,2880]{2,1,0:T(8,128)(2,1)} async-done(((bf16[32,16,2880]{2,1,0:T(8,128)(2,1)}), bf16[32,16,2880]{2,1,0:T(8,128)(2,1)}, u32[]{:S(2)}, u32[]{:S(2)}) %all-to-all-start.3) | async-done | bytes 2949152 | tf_op jit(solution)/shard_map/all_to_all | solution.py:151
  158.8 5.2 %fusion.19 = f32[32,1,16,360]{3,2,0,1:T(8,128)} fusion(bf16[32,16,2880]{2,1,0:T(8,128)(2,1)} %all-to-all-done.3, bf16[1,2880,360]{1,2,0:T(8,128)(2,1)} %param.25), kind=kOutput, calls=%fused_computation.31 | convolution fusion | flops 1061683200 | bytes 5760000 | tf_op jit(solution)/shard_map/sexd,edf->sexf/dot_general | solution.py:153
  164.0 8.6 %convolution_convert_fusion.3 = bf16[32,16,8,360]{3,1,0,2:T(8,128)(2,1)} fusion(bf16[360,8,360,1]{2,1,0,3:T(8,128)(2,1)} %bitcast.231, bf16[32,16,2880]{2,1,0:T(8,128)(2,1)} %all-to-all-done.3, bf16[1,2880,360]{1,2,0:T(8,128)(2,1)} %param.26, f32[32,1,16,360]{3,2,0,1:T(8,128)} %fusion.19), kind=kOutput, calls=%fused_computation.12 | convolution fusion | flops 2126315520 | bytes 10782720 | tf_op jit(solution)/shard_map/sexf,efjk->jsexk/dot_general | solution.py:172
  172.7 5.0 %copy.103 = bf16[512,8,360]{2,1,0:T(8,128)(2,1)} copy(bf16[512,8,360]{0,2,1:T(8,128)(2,1)} %bitcast.230) | data formatting | bytes 5898240 | tf_op jit(solution)/shard_map/transpose | solution.py:166
  177.7 6.4 %reshape.530 = bf16[32,16,2880]{2,1,0:T(8,128)(2,1)} reshape(bf16[512,8,360]{2,1,0:T(8,128)(2,1)} %copy.103) | data formatting | bytes 5898240 | tf_op jit(solution)/shard_map/reshape.58
  184.0 5.2 %fusion.22 = f32[32,1,16,360]{3,2,0,1:T(8,128)} fusion(bf16[32,16,2880]{2,1,0:T(8,128)(2,1)} %reshape.530, bf16[1,2880,360]{1,2,0:T(8,128)(2,1)} %param.25), kind=kOutput, calls=%fused_computation.32 | convolution fusion | flops 1061683200 | bytes 5760000 | tf_op jit(solution)/shard_map/sexd,edf->sexf/dot_general | solution.py:167
  189.3 8.7 %convolution_convert_fusion.2 = bf16[32,16,8,360]{3,1,0,2:T(8,128)(2,1)} fusion(bf16[360,8,360,1]{2,1,0,3:T(8,128)(2,1)} %bitcast.232, bf16[32,16,2880]{2,1,0:T(8,128)(2,1)} %reshape.530, bf16[1,2880,360]{1,2,0:T(8,128)(2,1)} %param.26, f32[32,1,16,360]{3,2,0,1:T(8,128)} %fusion.22), kind=kOutput, calls=%fused_computation.11 | convolution fusion | flops 2126315520 | bytes 10782720 | tf_op jit(solution)/shard_map/sexf,efjk->jsexk/dot_general | solution.py:172
  198.0 12.6 %reduce-scatter.3.cloned.1.call-done = bf16[512,360]{1,0:T(8,128)(2,1)} async-done(((bf16[4096,360]{1,0:T(8,128)(2,1)}), bf16[512,360]{1,0:T(8,128)(2,1)}) %reduce-scatter.3.cloned.1.call-update) | async-done | bytes 368656 | tf_op jit(solution)/shard_map/reduce_scatter | solution.py:177
  210.6 20.7 %all_to_all.37 = bf16[32,16,360]{2,1,0:T(8,128)(2,1)S(1)} all-to-all(bf16[32,16,360]{2,1,0:T(8,128)(2,1)} %bitcast.240), channel_id=1, replica_groups=mesh['seq'=32,'tp'=8] {'seq'}, dimensions={0} | all-to-all | bytes 737280 | tf_op jit(solution)/shard_map/all_to_all | solution.py:178
  231.3 28.3 %reduce-scatter.5.cloned.1.call-done = bf16[512,360]{1,0:T(8,128)(2,1)} async-done(((bf16[4096,360]{1,0:T(8,128)(2,1)}), bf16[512,360]{1,0:T(8,128)(2,1)}) %reduce-scatter.5.cloned.1.call-update) | async-done | bytes 368656 | tf_op jit(solution)/shard_map/reduce_scatter | solution.py:177
  259.6 10.7 %all-to-all-start.6 = ((bf16[32,16,360]{2,1,0:T(8,128)(2,1)}), bf16[32,16,360]{2,1,0:T(8,128)(2,1)}, u32[]{:S(2)}, u32[]{:S(2)}) async-start(bf16[32,16,360]{2,1,0:T(8,128)(2,1)} %bitcast.241), calls=%async_computation.8 | async-start | bytes 786432 | tf_op jit(solution)/shard_map/all_to_all | solution.py:178
  270.5 1.7 copy.107
  272.2 8.4 %all-to-all-done.6 = bf16[32,16,360]{2,1,0:T(8,128)(2,1)} async-done(((bf16[32,16,360]{2,1,0:T(8,128)(2,1)}), bf16[32,16,360]{2,1,0:T(8,128)(2,1)}, u32[]{:S(2)}, u32[]{:S(2)}) %all-to-all-start.6) | async-done | bytes 368672 | tf_op jit(solution)/shard_map/all_to_all | solution.py:178
  280.6 2.0 pad_maximum_fusion
  282.6 3.0 %gather_fusion.1 = bf16[512,360]{1,0:T(8,128)(2,1)S(1)} fusion(bf16[1024,360]{1,0:T(8,128)(2,1)} %bitcast.225, s32[1024]{0:T(1024)S(1)} %pad_clamp_fusion), kind=kCustom, calls=%fused_computation.1 | custom fusion | bytes 739328 | tf_op jit(solution)/shard_map/gather | solution.py:188
  286.8 1.7 multiply_reduce_fusion.1
  (81 shorter events, 16.5 us)
Async XLA Ops:
  7.2 26.3 %copy-start = (bf16[512,2880]{0,1:T(8,128)(2,1)S(1)}, bf16[512,2880]{0,1:T(8,128)(2,1)}, u32[]{:S(2)}) copy-start(bf16[512,2880]{0,1:T(8,128)(2,1)} %param.21) | copy-start | bytes 8847364
  10.4 18.6 %all-to-all-start = ((bf16[32,32,1,128]{3,1,2,0:T(8,128)(2,1)}), bf16[32,32,1,128]{3,1,2,0:T(8,128)(2,1)S(1)}, u32[]{:S(2)}, u32[]{:S(2)}) async-start(bf16[32,32,1,128]{3,1,2,0:T(8,128)(2,1)} %bitcast.5), calls=%async_computation | async-start | bytes 524288 | tf_op jit(solution)/shard_map/all_to_all | solution.py:68
  29.1 1.8 copy-start.6
  29.1 1.8 copy-start.10
  29.1 1.9 copy-start.7
  29.1 1.8 copy-start.1
  31.9 1.2 copy-start.4
  33.5 1.0 copy-start.2
  33.5 31.4 %copy-start.3 = (bf16[128,360]{0,1:T(8,128)(2,1)S(1)}, bf16[128,360]{0,1:T(8,128)(2,1)}, u32[]{:S(2)}) copy-start(bf16[128,360]{0,1:T(8,128)(2,1)} %param.14) | copy-start | bytes 276484
  34.4 35.7 %copy-start.8 = (s32[128,4]{0,1:T(4,128)S(1)}, s32[128,4]{0,1:T(4,128)}, u32[]{:S(2)}) copy-start(s32[128,4]{0,1:T(4,128)} %param.23) | copy-start | bytes 6148
  34.5 37.7 %copy-start.5 = (f32[2880]{0:T(1024)S(1)}, f32[2880]{0:T(1024)}, u32[]{:S(2)}) copy-start(f32[2880]{0:T(1024)} %param.22) | copy-start | bytes 34564
  65.9 26.7 %all-to-all-start.2 = ((bf16[8,128,360]{1,2,0:T(8,128)(2,1)}), bf16[8,128,360]{1,2,0:T(8,128)(2,1)}, u32[]{:S(2)}, u32[]{:S(2)}) async-start(bf16[8,128,360]{1,2,0:T(8,128)(2,1)} %broadcast_in_dim.49), calls=%async_computation.2 | async-start | bytes 1474560 | tf_op jit(solution)/shard_map/all_to_all | solution.py:115
  70.1 102.6 %all-gather.2.cloned.1.call-start = ((), (), s32[]{:S(2)}) async-start(), calls=%async_computation.10 | async-start | bytes 3317760 | tf_op jit(solution)/shard_map/all_gather | solution.py:163
  115.9 42.9 %all-to-all-start.3 = ((bf16[32,16,2880]{2,1,0:T(8,128)(2,1)}), bf16[32,16,2880]{2,1,0:T(8,128)(2,1)}, u32[]{:S(2)}, u32[]{:S(2)}) async-start(bf16[32,16,2880]{2,1,0:T(8,128)(2,1)} %bitcast.226), calls=%async_computation.3 | async-start | bytes 6029312 | tf_op jit(solution)/shard_map/all_to_all | solution.py:151
  120.6 90.0 %reduce-scatter.3.cloned.1.call-start = ((), (), s32[]{:S(2)}) async-start(), calls=%async_computation.9 | async-start | bytes 3538944 | tf_op jit(solution)/shard_map/reduce_scatter | solution.py:177
  172.6 87.0 %reduce-scatter.5.cloned.1.call-start = ((), (), s32[]{:S(2)}) async-start(), calls=%async_computation.11 | async-start | bytes 3538944 | tf_op jit(solution)/shard_map/reduce_scatter | solution.py:177
  198.0 72.4 %copy-start.9 = (f32[128,4]{0,1:T(4,128)S(1)}, f32[128,4]{0,1:T(4,128)}, u32[]{:S(2)}) copy-start(f32[128,4]{0,1:T(4,128)} %param.24) | copy-start | bytes 6148
  259.6 21.0 %all-to-all-start.6 = ((bf16[32,16,360]{2,1,0:T(8,128)(2,1)}), bf16[32,16,360]{2,1,0:T(8,128)(2,1)}, u32[]{:S(2)}, u32[]{:S(2)}) async-start(bf16[32,16,360]{2,1,0:T(8,128)(2,1)} %bitcast.241), calls=%async_computation.8 | async-start | bytes 786432 | tf_op jit(solution)/shard_map/all_to_all | solution.py:178
Sparse Core Ops, SparseCore 0:
  111.9 34.3 all-gather.1
  172.7 37.8 reduce-scatter.2
  213.1 46.4 reduce-scatter.4

commit v8 on v5

--- a/solution.py
+++ b/solution.py
@@ -121,25 +121,29 @@
     local_e = w_gate.shape[0]
     experts_all = local_e * seq_count
     cap = 2 * rows * topk // experts_all
-    chunks = 2
-    part = cap // chunks
+    bounds = (0, 20, cap)
     flat_routes = routes.reshape(-1)
     onehot = (flat_routes[:, None] == jnp.arange(experts_all, dtype=jnp.int32)[None, :]).astype(
         jnp.int32
     )
     rank = jnp.sum(onehot * (jnp.cumsum(onehot, 0) - 1), 1)
-    slot = (rank // part) * (experts_all * part) + flat_routes * part + rank % part
+    slot = jnp.zeros_like(rank)
+    for lo, hi in zip(bounds[:-1], bounds[1:]):
+        inside = (rank >= lo) & (rank < hi)
+        slot = jnp.where(inside, experts_all * lo + flat_routes * (hi - lo) + rank - lo, slot)
     source = (
         jnp.full((experts_all * cap,), rows, jnp.int32)
         .at[slot]
         .set(jnp.arange(rows * topk, dtype=jnp.int32) // topk)
-    ).reshape(chunks, experts_all * part)
+    )
     token_ids = jnp.arange(rows, dtype=jnp.int32)
     w_down_split = w_down.reshape(local_e, w_down.shape[1], tp_count, cols)
     row_major2 = Layout(major_to_minor=(0, 1))
     pieces = []
-    for c in range(chunks):
-        picks = (source[c][:, None] == token_ids[None, :]).astype(jnp.bfloat16)
+    for lo, hi in zip(bounds[:-1], bounds[1:]):
+        part = hi - lo
+        chunk_src = source[experts_all * lo:experts_all * hi]
+        picks = (chunk_src[:, None] == token_ids[None, :]).astype(jnp.bfloat16)
         sent = jnp.dot(picks, normed_full, preferred_element_type=jnp.float32).astype(
             jnp.bfloat16
         )
@@ -163,12 +167,8 @@
             tiled=True,
         )
         pieces.append(back)
-    returned = jnp.stack(pieces, 0)
-    taken = (
-        returned.reshape(experts_all * cap, cols)[slot]
-        .reshape(rows, topk, cols)
-        .astype(jnp.float32)
-    )
+    returned = jnp.concatenate([p.reshape(-1, cols) for p in pieces], 0)
+    taken = returned[slot].reshape(rows, topk, cols).astype(jnp.float32)
     mixture = jnp.sum(route_wt[..., None] * taken, 1)
     output = (resid_wide + mixture).astype(jnp.bfloat16)
     return (attended, output)

time: 291 us -> 319 us (1.096)
  blocking collectives: 73.7 us -> 30.5 us
  waiting for transfers between devices: 91.4 us -> 125 us
  local copies, waits for them, and re-layouts: 25.2 us -> 58.3 us
  starting transfers between devices: 34.3 us -> 40.7 us
  other arithmetic: 14.1 us -> 10.9 us
    all_to_all x1 -> x0, blocking collectives: 43.4 us -> none  [per_device(): lax.all_to_all(sent, 'seq', split_axis=0, concat_axis=0, tiled=True)]
    reshape x0 -> x8, local copies, waits for them, and re-layouts: none -> 25.6 us  [the longest x2 12.7 us: per_device(): down = down.reshape(tp_count * seq_count * local_e * part, cols)]
    all_to_all x1 -> x2, waiting for transfers between devices: 32.7 us -> 57.7 us  [per_device(): lax.all_to_all(sent, 'seq', split_axis=0, concat_axis=0, tiled=True)]
    all_to_all x1 -> x2, starting transfers between devices: 6.36 us -> 13.4 us  [per_device(): lax.all_to_all(sent, 'seq', split_axis=0, concat_axis=0, tiled=True)]
    reduce_scatter x2, waiting for transfers between devices: 32.4 us -> 38.5 us  [per_device(): expert_out = lax.psum_scatter(down, 'tp', scatter_dimension=0, tiled=True)]
    dot_general x0 -> x2, local copies, waits for them, and re-layouts: none -> 5.44 us  [per_device(): jnp.einsum('sexf,efjk->jsexk', act, w_down_split, preferred_element_type=...]
    convert_element_type x1 -> x3, local copies, waits for them, and re-layouts: 1.09 us -> 6.22 us  [the longest x2 5.14 us: per_device(): down = jnp.einsum('sexf,efjk->jsexk', act, w_down_split, preferred_elemen...]
  transfers between devices with their start and end apart: 7 -> 8, of which waited for: 4 -> 5; matrix products, arithmetic and copies ran while one was open for 12% -> 27% of each run, Pallas kernels for 0% -> 0%
where the time goes in v8:
time: 319 us; the launch traced here: 318 us
  waiting for transfers between devices  125 us (39%)
  local copies, waits for them, and re-layouts  58.3 us (18%)
  starting transfers between devices  40.7 us (13%)
  matrix products  38 us (12%)
  blocking collectives  30.5 us (10%)
  between operations  14.5 us (5%)
  other arithmetic  10.9 us (3%)
    all_to_all x2, waiting for transfers between devices, per_device(): lax.all_to_all(sent, 'seq', split_axis=0, concat_axis=0, tiled=True)  57.7 us
    reduce_scatter x2, waiting for transfers between devices, per_device(): expert_out = lax.psum_scatter(down, 'tp', scatter_dimension=0, tiled=True)  38.5 us
    all_to_all x1, blocking collectives, per_device(): lax.all_to_all(blocks, 'tp', split_axis=0, concat_axis=0, tiled=True)  30.5 us
    all_to_all x1, waiting for transfers between devices, per_device(): lax.all_to_all(spread, 'tp', split_axis=0, concat_axis=0, tiled=True)  17.6 us
    dot_general x2, matrix products, per_device(): jnp.einsum('sexf,efjk->jsexk', act, w_down_split, preferred_element_type=...  17.3 us
    all_to_all x2, starting transfers between devices, per_device(): lax.all_to_all(expert_out.reshape(seq_count, local_e * part, cols), 'seq'...  15.1 us
    all_to_all x2, starting transfers between devices, per_device(): lax.all_to_all(sent, 'seq', split_axis=0, concat_axis=0, tiled=True)  13.4 us
    reshape x2, local copies, waits for them, and re-layouts, per_device(): down = down.reshape(tp_count * seq_count * local_e * part, cols)  12.7 us
  transfers between devices with their start and end apart: 8, of which 5 were waited for; matrix products, arithmetic and copies ran while one was open for 27% of the time, Pallas kernels for 0%

profile of v8, /device:TPU:1, one launch (start us, length us, event | category | flops | bytes accessed | tf_op | source)
XLA Modules:
  0.0 317.8 jit_solution(9894665109005006257)
XLA Ops:
  8.2 2.2 gather_fusion
  10.4 8.6 %all-to-all-start = ((bf16[32,32,1,128]{3,1,2,0:T(8,128)(2,1)}), bf16[32,32,1,128]{3,1,2,0:T(8,128)(2,1)S(1)}, u32[]{:S(2)}, u32[]{:S(2)}) async-start(bf16[32,32,1,128]{3,1,2,0:T(8,128)(2,1)} %bitcast.5), calls=%async_computation | async-start | bytes 524288 | tf_op jit(solution)/shard_map/all_to_all | solution.py:68
  26.6 2.5 fusion.145
  34.4 30.5 %all_to_all.35 = bf16[8,128,360]{1,2,0:T(8,128)(2,1)S(1)} all-to-all(bf16[8,128,360]{1,2,0:T(8,128)(2,1)S(1)} %bitcast.227), channel_id=1, replica_groups=mesh['seq'=32,'tp'=8] {'tp'}, dimensions={0} | all-to-all | bytes 1474560 | tf_op jit(solution)/shard_map/all_to_all | solution.py:110
  66.0 3.5 %all-to-all-start.2 = ((bf16[8,128,360]{1,2,0:T(8,128)(2,1)}), bf16[8,128,360]{1,2,0:T(8,128)(2,1)S(1)}, u32[]{:S(2)}, u32[]{:S(2)}) async-start(bf16[8,128,360]{1,2,0:T(8,128)(2,1)} %broadcast_in_dim.49), calls=%async_computation.2 | async-start | bytes 1474560 | tf_op jit(solution)/shard_map/all_to_all | solution.py:115
  71.9 2.4 scatter_custom_fusion
  74.4 17.6 %all-to-all-done.2 = bf16[8,128,360]{1,2,0:T(8,128)(2,1)S(1)} async-done(((bf16[8,128,360]{1,2,0:T(8,128)(2,1)}), bf16[8,128,360]{1,2,0:T(8,128)(2,1)S(1)}, u32[]{:S(2)}, u32[]{:S(2)}) %all-to-all-start.2) | async-done | bytes 737312 | tf_op jit(solution)/shard_map/all_to_all | solution.py:115
  94.6 2.3 reshape.501
  96.9 6.4 %all-to-all-start.5 = ((bf16[32,12,2880]{2,1,0:T(8,128)(2,1)}), bf16[32,12,2880]{2,1,0:T(8,128)(2,1)}, u32[]{:S(2)}, u32[]{:S(2)}) async-start(bf16[32,12,2880]{2,1,0:T(8,128)(2,1)} %reshape.501), calls=%async_computation.6 | async-start | bytes 6029312 | tf_op jit(solution)/shard_map/all_to_all | solution.py:151
  103.3 4.7 %reshape.497 = bf16[360,8,360]{2,1,0:T(8,128)(2,1)S(1)} reshape(bf16[1,360,2880]{2,1,0:T(8,128)(2,1)} %param.27) | data formatting | bytes 4147200 | tf_op jit(solution)/shard_map/reshape.50
  108.1 3.1 convolution_convert_fusion
  111.2 6.5 %reshape.493 = bf16[32,20,2880]{2,1,0:T(8,128)(2,1)} reshape(bf16[640,2880]{1,0:T(8,128)(2,1)} %convolution_convert_fusion) | data formatting | bytes 7372800 | tf_op jit(solution)/shard_map/reshape | solution.py:150
  117.6 24.2 %all-to-all-done.5 = bf16[32,12,2880]{2,1,0:T(8,128)(2,1)} async-done(((bf16[32,12,2880]{2,1,0:T(8,128)(2,1)}), bf16[32,12,2880]{2,1,0:T(8,128)(2,1)}, u32[]{:S(2)}, u32[]{:S(2)}) %all-to-all-start.5) | async-done | bytes 2211872 | tf_op jit(solution)/shard_map/all_to_all | solution.py:151
  141.8 7.0 %all-to-all-start.3 = ((bf16[32,20,2880]{2,1,0:T(8,128)(2,1)}), bf16[32,20,2880]{2,1,0:T(8,128)(2,1)}, u32[]{:S(2)}, u32[]{:S(2)}) async-start(bf16[32,20,2880]{2,1,0:T(8,128)(2,1)} %reshape.493), calls=%async_computation.3 | async-start | bytes 9043968 | tf_op jit(solution)/shard_map/all_to_all | solution.py:151
  148.8 3.9 %fusion.43 = f32[32,1,12,360]{3,0,2,1:T(8,128)S(1)} fusion(bf16[1,2880,360]{1,2,0:T(8,128)(2,1)} %param.25, bf16[32,12,2880]{2,1,0:T(8,128)(2,1)} %all-to-all-done.5), kind=kOutput, calls=%fused_computation.46 | convolution fusion | flops 796262400 | bytes 4838400 | tf_op jit(solution)/shard_map/sexd,edf->sexf/dot_general | solution.py:153
  152.7 6.6 %fusion.3 = bf16[32,12,8,360]{3,0,2,1:T(8,128)(2,1)} fusion(bf16[360,8,360]{2,1,0:T(8,128)(2,1)S(1)} %reshape.497, bf16[1,2880,360]{1,2,0:T(8,128)(2,1)} %param.26, bf16[32,12,2880]{2,1,0:T(8,128)(2,1)} %all-to-all-done.5, f32[32,1,12,360]{3,0,2,1:T(8,128)S(1)} %fusion.43), kind=kOutput, calls=%fused_computation.16 | convolution fusion | flops 1593630720 | bytes 9123840 | tf_op jit(solution)/shard_map/sexf,efjk->jsexk/dot_general | solution.py:156
  159.3 2.5 copy.170
  161.8 2.1 copy.172
  163.9 5.3 %reshape.503 = bf16[3072,360]{1,0:T(8,128)(2,1)} reshape(bf16[8,32,1,12,360]{4,3,2,1,0:T(8,128)(2,1)} %bitcast.226) | data formatting | bytes 4423680 | tf_op jit(solution)/shard_map/reshape | solution.py:160
  169.3 33.5 %all-to-all-done.3 = bf16[32,20,2880]{2,1,0:T(8,128)(2,1)} async-done(((bf16[32,20,2880]{2,1,0:T(8,128)(2,1)}), bf16[32,20,2880]{2,1,0:T(8,128)(2,1)}, u32[]{:S(2)}, u32[]{:S(2)}) %all-to-all-start.3) | async-done | bytes 3686432 | tf_op jit(solution)/shard_map/all_to_all | solution.py:151
  202.9 6.6 %fusion.25 = f32[32,1,20,360]{3,2,0,1:T(8,128)} fusion(bf16[32,20,2880]{2,1,0:T(8,128)(2,1)} %all-to-all-done.3, bf16[1,2880,360]{1,2,0:T(8,128)(2,1)} %param.25), kind=kOutput, calls=%fused_computation.40 | convolution fusion | flops 1327104000 | bytes 6681600 | tf_op jit(solution)/shard_map/sexd,edf->sexf/dot_general | solution.py:153
  209.5 10.6 %fusion.5 = bf16[32,20,8,360]{3,1,2,0:T(8,128)(2,1)} fusion(bf16[360,8,360]{2,1,0:T(8,128)(2,1)S(1)} %copy-done.5, bf16[32,20,2880]{2,1,0:T(8,128)(2,1)} %all-to-all-done.3, bf16[1,2880,360]{1,2,0:T(8,128)(2,1)} %param.26, f32[32,1,20,360]{3,2,0,1:T(8,128)} %fusion.25), kind=kOutput, calls=%fused_computation.18 | convolution fusion | flops 2656051200 | bytes 12441600 | tf_op jit(solution)/shard_map/sexf,efjk->jsexk/dot_general | solution.py:156
  220.1 2.9 copy.169
  223.0 3.0 copy.171
  226.1 7.3 %reshape.498 = bf16[5120,360]{1,0:T(8,128)(2,1)} reshape(bf16[8,32,1,20,360]{4,3,2,1,0:T(8,128)(2,1)} %bitcast.225) | data formatting | bytes 7372800 | tf_op jit(solution)/shard_map/reshape | solution.py:160
  233.5 1.8 reshape.504
  235.3 7.5 %all-to-all-start.6 = ((bf16[32,12,360]{2,1,0:T(8,128)(2,1)}), bf16[32,12,360]{2,1,0:T(8,128)(2,1)S(1)}, u32[]{:S(2)}, u32[]{:S(2)}) async-start(bf16[32,12,360]{2,1,0:T(8,128)(2,1)} %reshape.504), calls=%async_computation.8 | async-start | bytes 786432 | tf_op jit(solution)/shard_map/all_to_all | solution.py:162
  242.8 38.5 %reduce-scatter.3.cloned.1.call-done = bf16[640,360]{1,0:T(8,128)(2,1)} async-done(((bf16[5120,360]{1,0:T(8,128)(2,1)}), bf16[640,360]{1,0:T(8,128)(2,1)}) %reduce-scatter.3.cloned.1.call-update) | async-done | bytes 460816 | tf_op jit(solution)/shard_map/reduce_scatter | solution.py:161
  281.3 2.0 reshape.499
  283.3 7.6 %all-to-all-start.4 = ((bf16[32,20,360]{2,1,0:T(8,128)(2,1)}), bf16[32,20,360]{2,1,0:T(8,128)(2,1)S(1)}, u32[]{:S(2)}, u32[]{:S(2)}) async-start(bf16[32,20,360]{2,1,0:T(8,128)(2,1)} %reshape.499), calls=%async_computation.5 | async-start | bytes 1179648 | tf_op jit(solution)/shard_map/all_to_all | solution.py:162
  291.9 11.1 %all-to-all-done.4 = bf16[32,20,360]{2,1,0:T(8,128)(2,1)S(1)} async-done(((bf16[32,20,360]{2,1,0:T(8,128)(2,1)}), bf16[32,20,360]{2,1,0:T(8,128)(2,1)S(1)}, u32[]{:S(2)}, u32[]{:S(2)}) %all-to-all-start.4) | async-done | bytes 460832 | tf_op jit(solution)/shard_map/all_to_all | solution.py:162
  304.2 3.2 %gather_fusion.1 = bf16[512,360]{1,0:T(8,128)(2,1)S(1)} fusion(bf16[1024,360]{1,0:T(8,128)(2,1)} %pad_maximum_fusion, s32[1024]{0:T(1024)S(1)} %pad_clamp_fusion), kind=kCustom, calls=%fused_computation.1 | custom fusion | bytes 739328 | tf_op jit(solution)/shard_map/gather | solution.py:171
  (98 shorter events, 25.6 us)
Async XLA Ops:
  7.2 26.3 %copy-start = (bf16[512,2880]{0,1:T(8,128)(2,1)S(1)}, bf16[512,2880]{0,1:T(8,128)(2,1)}, u32[]{:S(2)}) copy-start(bf16[512,2880]{0,1:T(8,128)(2,1)} %param.21) | copy-start | bytes 8847364
  10.4 18.6 %all-to-all-start = ((bf16[32,32,1,128]{3,1,2,0:T(8,128)(2,1)}), bf16[32,32,1,128]{3,1,2,0:T(8,128)(2,1)S(1)}, u32[]{:S(2)}, u32[]{:S(2)}) async-start(bf16[32,32,1,128]{3,1,2,0:T(8,128)(2,1)} %bitcast.5), calls=%async_computation | async-start | bytes 524288 | tf_op jit(solution)/shard_map/all_to_all | solution.py:68
  29.2 1.6 copy-start.9
  29.2 1.6 copy-start.14
  29.2 1.7 copy-start.11
  31.8 1.2 copy-start.6
  31.8 1.3 copy-start.8
  34.4 30.6 %copy-start.7 = (bf16[128,360]{0,1:T(8,128)(2,1)S(1)}, bf16[128,360]{0,1:T(8,128)(2,1)}, u32[]{:S(2)}) copy-start(bf16[128,360]{0,1:T(8,128)(2,1)} %param.14) | copy-start | bytes 276484
  34.4 35.1 %copy-start.12 = (s32[128,4]{0,1:T(4,128)S(1)}, s32[128,4]{0,1:T(4,128)}, u32[]{:S(2)}) copy-start(s32[128,4]{0,1:T(4,128)} %param.23) | copy-start | bytes 6148
  65.0 27.4 %copy-start.10 = (f32[2880]{0:T(1024)S(1)}, f32[2880]{0:T(1024)}, u32[]{:S(2)}) copy-start(f32[2880]{0:T(1024)} %param.22) | copy-start | bytes 34564
  66.0 26.0 %all-to-all-start.2 = ((bf16[8,128,360]{1,2,0:T(8,128)(2,1)}), bf16[8,128,360]{1,2,0:T(8,128)(2,1)S(1)}, u32[]{:S(2)}, u32[]{:S(2)}) async-start(bf16[8,128,360]{1,2,0:T(8,128)(2,1)} %broadcast_in_dim.49), calls=%async_computation.2 | async-start | bytes 1474560 | tf_op jit(solution)/shard_map/all_to_all | solution.py:115
  92.9 0.9 copy-start.2
  96.9 44.9 %all-to-all-start.5 = ((bf16[32,12,2880]{2,1,0:T(8,128)(2,1)}), bf16[32,12,2880]{2,1,0:T(8,128)(2,1)}, u32[]{:S(2)}, u32[]{:S(2)}) async-start(bf16[32,12,2880]{2,1,0:T(8,128)(2,1)} %reshape.501), calls=%async_computation.6 | async-start | bytes 6029312 | tf_op jit(solution)/shard_map/all_to_all | solution.py:151
  103.3 4.8 %copy-start.3 = (bf16[128,2880]{0,1:T(8,128)(2,1)S(1)}, bf16[128,2880]{0,1:T(8,128)(2,1)}, u32[]{:S(2)}) copy-start(bf16[128,2880]{0,1:T(8,128)(2,1)} %copy-done.2) | copy-start | bytes 2211844
  108.0 44.6 %copy-start.4 = (bf16[360,8,360]{2,1,0:T(8,128)(2,1)}, bf16[360,8,360]{2,1,0:T(8,128)(2,1)S(1)}, u32[]{:S(2)}) copy-start(bf16[360,8,360]{2,1,0:T(8,128)(2,1)S(1)} %reshape.497) | copy-start | bytes 6220804
  141.8 61.1 %all-to-all-start.3 = ((bf16[32,20,2880]{2,1,0:T(8,128)(2,1)}), bf16[32,20,2880]{2,1,0:T(8,128)(2,1)}, u32[]{:S(2)}, u32[]{:S(2)}) async-start(bf16[32,20,2880]{2,1,0:T(8,128)(2,1)} %reshape.493), calls=%async_computation.3 | async-start | bytes 9043968 | tf_op jit(solution)/shard_map/all_to_all | solution.py:151
  148.8 84.7 %reduce-scatter.5.cloned.1.call-start = ((), (), s32[]{:S(2)}) async-start(), calls=%async_computation.10 | async-start | bytes 2654208 | tf_op jit(solution)/shard_map/reduce_scatter | solution.py:161
  169.3 40.2 %copy-start.5 = (bf16[360,8,360]{2,1,0:T(8,128)(2,1)S(1)}, bf16[360,8,360]{2,1,0:T(8,128)(2,1)}, u32[]{:S(2)}) copy-start(bf16[360,8,360]{2,1,0:T(8,128)(2,1)} %copy-done.4) | copy-start | bytes 6220804
  169.3 112.0 %reduce-scatter.3.cloned.1.call-start = ((), (), s32[]{:S(2)}) async-start(), calls=%async_computation.9 | async-start | bytes 4423680 | tf_op jit(solution)/shard_map/reduce_scatter | solution.py:161
  233.4 57.4 %copy-start.13 = (f32[128,4]{0,1:T(4,128)S(1)}, f32[128,4]{0,1:T(4,128)}, u32[]{:S(2)}) copy-start(f32[128,4]{0,1:T(4,128)} %param.24) | copy-start | bytes 6148
  235.3 48.0 %all-to-all-start.6 = ((bf16[32,12,360]{2,1,0:T(8,128)(2,1)}), bf16[32,12,360]{2,1,0:T(8,128)(2,1)S(1)}, u32[]{:S(2)}, u32[]{:S(2)}) async-start(bf16[32,12,360]{2,1,0:T(8,128)(2,1)} %reshape.504), calls=%async_computation.8 | async-start | bytes 786432 | tf_op jit(solution)/shard_map/all_to_all | solution.py:162
  283.3 19.7 %all-to-all-start.4 = ((bf16[32,20,360]{2,1,0:T(8,128)(2,1)}), bf16[32,20,360]{2,1,0:T(8,128)(2,1)S(1)}, u32[]{:S(2)}, u32[]{:S(2)}) async-start(bf16[32,20,360]{2,1,0:T(8,128)(2,1)} %reshape.499), calls=%async_computation.5 | async-start | bytes 1179648 | tf_op jit(solution)/shard_map/all_to_all | solution.py:162
  304.2 6.8 %copy-start.1 = (bf16[512,2880]{0,1:T(8,128)(2,1)S(1)}, bf16[512,2880]{0,1:T(8,128)(2,1)}, u32[]{:S(2)}) copy-start(bf16[512,2880]{0,1:T(8,128)(2,1)} %param.21) | copy-start | bytes 8847364
Sparse Core Ops, SparseCore 0:
  169.4 35.2 reduce-scatter.4
  233.6 47.6 reduce-scatter.2
